TPU v7x, 512 devices: a whole 4x4x16 slice. The times are simulated.
512 devices in a mesh: section: 64 (over z, y_hi, core), expert: 8 (over x, y_lo).
Axes of the slice: x: 4, y: 4 (y_hi: 2, y_lo: 2; y = y_hi * 2 + y_lo), z: 16, core: 2. Of those that a mesh axis runs over, the one named last changes fastest.
Arguments:
- tokens: bfloat16 [65536, 2048], P(('section', 'expert')), may hold values from -6 to 6
- routes: int32 [2, 65536, 2], P(None, ('section', 'expert')), may hold values from 0 to 7, all different within a row; in each aligned block of 128 rows (0 to 127, 128 to 255, ..., all dimensions but the last counted through in order) at most 36 rows name the same one
- combine: float32 [2, 65536, 2], P(None, ('section', 'expert')), may hold values from 0.25 to 4
- up_weight: bfloat16 [64, 8, 2048, 512], P('section', 'expert'), may hold values from -0.125 to 0.125
- down_weight: bfloat16 [64, 8, 512, 2048], P('section', 'expert'), may hold values from -0.1875 to 0.1875
Outputs:
- mixed: bfloat16 [65536, 2048], P(('section', 'expert'))
Inputs may be any that keep to these rules, and one draw needn't show every extreme that they name: `routes`: each row names 2 different experts; among the rows of one device at one stop, no expert is named by more than 36 rows, a bound that some block reaches.
All inputs are finite; a program needn't handle non-finite values.
Results may differ from a plain program's by a relative error of at most 0.0061.
Values may be sent and summed in bfloat16 or wider, within the bound.
No kernel may reach another device: no remote copies, remote signals or barrier semaphores. Data moves between devices by JAX's collectives and lax.ppermute only.
A program may use at most 64 MiB of HBM per device.

v0:
```python
import jax
import jax.numpy as jnp
from jax import lax
from jax.sharding import PartitionSpec as P

TICKS = 2


def swapped(value, axis, distance):
    mask = 2**distance
    pairs = [(source, source ^ mask) for source in range(lax.axis_size(axis))]
    return lax.ppermute(value, axis, pairs)


def shifted(value, axis, steps):
    count = lax.axis_size(axis)
    pairs = [(source, (source + steps) % count) for source in range(count)]
    return lax.ppermute(value, axis, pairs)


def expert_half(rows, up_part, down_part):
    hidden = jax.nn.gelu(
        jnp.dot(rows, up_part, preferred_element_type=jnp.float32), approximate=True
    ).astype(jnp.bfloat16)
    return jnp.dot(hidden, down_part, preferred_element_type=jnp.float32).astype(jnp.bfloat16)


def body(tokens, routes, combine, up_weight, down_weight):
    rows = tokens.shape[0]
    width = tokens.shape[1]
    top = routes.shape[2]
    groups = lax.axis_size("expert")
    slots = min(rows, rows * top * 9 // (8 * groups))
    up_local = up_weight.reshape(up_weight.shape[2], up_weight.shape[3])
    down_local = down_weight.reshape(down_weight.shape[2], down_weight.shape[3])
    partner_up, partner_down = swapped((up_local, down_local), "section", 0)
    state = tokens
    for tick in range(TICKS):
        if tick > 0:
            state = shifted(state, "section", 2)
        ids = routes[tick]
        weights = combine[tick]
        state_f = state.astype(jnp.float32)
        normed = (
            state_f * lax.rsqrt(jnp.mean(state_f * state_f, axis=1, keepdims=True) + 1e-06)
        ).astype(jnp.bfloat16)
        share = weights / jnp.sum(weights, axis=1, keepdims=True)
        flat_ids = ids.reshape(-1)
        chosen = (flat_ids[:, None] == jnp.arange(groups, dtype=jnp.int32)[None, :]).astype(
            jnp.int32
        )
        before = jnp.cumsum(chosen, axis=0) - chosen
        position = jnp.sum(before * chosen, axis=1)
        target = flat_ids * slots + position
        anchor = (
            jnp.zeros((groups * slots,), jnp.int32)
            .at[target]
            .set(jnp.arange(rows * top, dtype=jnp.int32) // top)
        )
        filled = jnp.zeros((groups * slots,), jnp.bool_).at[target].set(True)
        outgoing = jnp.where(filled[:, None], normed[anchor], jnp.zeros((), jnp.bfloat16)).reshape(
            groups, slots, width
        )
        received = lax.all_to_all(
            outgoing, "expert", split_axis=0, concat_axis=0, tiled=True
        ).reshape(groups * slots, width)
        own_part = lax.optimization_barrier(expert_half(received, up_local, down_local))
        other_part = lax.optimization_barrier(expert_half(received, partner_up, partner_down))
        summed = own_part.astype(jnp.float32) + other_part.astype(jnp.float32)
        expert_out = summed.astype(jnp.bfloat16).reshape(groups, slots, width)
        answers = lax.all_to_all(
            expert_out, "expert", split_axis=0, concat_axis=0, tiled=True
        ).reshape(groups * slots, width)
        gathered = answers[target].astype(jnp.float32).reshape(rows, top, width)
        state = (state_f + jnp.sum(gathered * share[:, :, None], axis=1)).astype(jnp.bfloat16)
    return state


def solution(mesh):
    in_specs = (
        P(("section", "expert"), None),
        P(None, ("section", "expert"), None),
        P(None, ("section", "expert"), None),
        P("section", "expert", None, None),
        P("section", "expert", None, None),
    )
    out_specs = P(("section", "expert"), None)
    return jax.shard_map(body, mesh=mesh, in_specs=in_specs, out_specs=out_specs, check_vma=False)
```

profile of v0, /device:TPU:2, one launch (start us, length us, event | category | flops | bytes accessed | tf_op | source)
XLA Modules:
  0.0 165.8 jit_solution(6728091189853279568)
XLA Ops:
  0.0 1.9 %collective-permute-start.1 = (bf16[512,2048]{1,0:T(8,128)(2,1)}, bf16[512,2048]{1,0:T(8,128)(2,1)}, u32[]{:S(2)}, u32[]{:S(2)}) collective-permute-start(bf16[512,2048]{1,0:T(8,128)(2,1)} %bitcast.58), channel_id=1, source_target_pairs={{0,8},{8,0},{16,24},{24,16},{32,40},{40,32},{48,56},{56,48},{64,72... | collective-permute-start | bytes 6291464 | tf_op jit(solution)/shard_map/ppermute | solution.py:12
  1.9 2.4 %collective-permute-start = (bf16[2048,512]{1,0:T(8,128)(2,1)}, bf16[2048,512]{1,0:T(8,128)(2,1)}, u32[]{:S(2)}, u32[]{:S(2)}) collective-permute-start(bf16[2048,512]{1,0:T(8,128)(2,1)} %bitcast.59), channel_id=1, source_target_pairs={{0,8},{8,0},{16,24},{24,16},{32,40},{40,32},{48,56},{56,48},{64,72... | collective-permute-start | bytes 6291464 | tf_op jit(solution)/shard_map/ppermute | solution.py:12
  5.5 1.2 fusion
  6.7 1.2 fusion.1
  9.1 1.4 scatter_custom_fusion.1
  10.5 2.4 %gather_fusion = bf16[288,2048]{1,0:T(8,128)(2,1)S(1)} fusion(bf16[128,2048]{1,0:T(8,128)(2,1)S(1)} %fusion.1, s32[1024]{0:T(1024)S(1)} %pad_clamp_fusion.3), kind=kCustom, calls=%fused_computation | custom fusion | bytes 2360448 | tf_op jit(solution)/shard_map/gather | solution.py:61
  13.9 1.5 scatter_custom_fusion
  15.6 25.2 %all_to_all.20 = bf16[8,36,2048]{2,1,0:T(8,128)(2,1)S(1)} all-to-all(bf16[8,36,2048]{2,1,0:T(8,128)(2,1)S(1)} %broadcast_select_fusion.1), channel_id=1, replica_groups=mesh['section'=64,'expert'=8] {'expert'}, dimensions={0} | all-to-all | bytes 2359296 | tf_op jit(solution)/shard_map/all_to_all | solution.py:64
  41.1 4.2 %convolution_convert_fusion.3 = bf16[288,2048]{1,0:T(8,128)(2,1)S(1)} fusion(bf16[1,1,512,2048]{3,2,1,0:T(8,128)(2,1)} %param.9, bf16[288,2048]{1,0:T(8,128)(2,1)S(1)} %reshape.195, bf16[1,1,2048,512]{3,2,1,0:T(8,128)(2,1)} %param.8), kind=kOutput, calls=%fused_computation.11 | convolution fusion | flops 1209876480 | bytes 6553600 | tf_op jit(solution)/shard_map/dot_general | solution.py:25
  45.4 4.1 %convolution_convert_fusion.2 = bf16[288,2048]{1,0:T(8,128)(2,1)S(1)} fusion(bf16[512,2048]{1,0:T(8,128)(2,1)} %collective-permute-done.1, bf16[288,2048]{1,0:T(8,128)(2,1)} %copy-done.1, bf16[2048,512]{1,0:T(8,128)(2,1)} %collective-permute-done), kind=kOutput, calls=%fused_computation.10 | convolution fusion | flops 1209876480 | bytes 6553600 | tf_op jit(solution)/shard_map/dot_general | solution.py:25
  50.0 1.2 reshape.198
  51.2 5.3 %all-to-all-start.1 = ((bf16[8,36,2048]{2,1,0:T(8,128)(2,1)}), bf16[8,36,2048]{2,1,0:T(8,128)(2,1)S(1)}, u32[]{:S(2)}, u32[]{:S(2)}) async-start(bf16[8,36,2048]{2,1,0:T(8,128)(2,1)} %reshape.198), calls=%async_computation.1 | async-start | bytes 2621440 | tf_op jit(solution)/shard_map/all_to_all | solution.py:71
  58.9 14.1 %all-to-all-done.1 = bf16[8,36,2048]{2,1,0:T(8,128)(2,1)S(1)} async-done(((bf16[8,36,2048]{2,1,0:T(8,128)(2,1)}), bf16[8,36,2048]{2,1,0:T(8,128)(2,1)S(1)}, u32[]{:S(2)}, u32[]{:S(2)}) %all-to-all-start.1) | async-done | bytes 1179680 | tf_op jit(solution)/shard_map/all_to_all | solution.py:71
  73.2 1.4 gather_fusion.1
  74.6 1.3 reshape.204
  76.0 3.2 %multiply_reduce_fusion.1 = f32[128,2048]{1,0:T(8,128)S(1)} fusion(f32[128,2,2048]{2,1,0:T(2,128)S(1)} %reshape.204, f32[128,2]{1,0:T(8,128)S(1)} %copy-done.2), kind=kLoop, calls=%fused_computation.15 | loop fusion | flops 786432 | bytes 3146752 | tf_op jit(solution)/shard_map/reduce_sum | solution.py:75
  79.3 1.9 %collective-permute-start.2 = (bf16[128,2048]{1,0:T(8,128)(2,1)S(1)}, bf16[128,2048]{1,0:T(8,128)(2,1)S(1)}, u32[]{:S(2)}, u32[]{:S(2)}) collective-permute-start(bf16[128,2048]{1,0:T(8,128)(2,1)S(1)} %fusion.2), channel_id=1, source_target_pairs={{0,16},{8,24},{16,32},{24,40},{32,48},{40,56},{48,64},{56,72},{64,... | collective-permute-start | bytes 1572872 | tf_op jit(solution)/shard_map/ppermute | solution.py:18
  81.2 1.6 scatter_custom_fusion.3
  82.8 1.6 scatter_custom_fusion.2
  84.5 16.2 %collective-permute-done.2 = bf16[128,2048]{1,0:T(8,128)(2,1)S(1)} collective-permute-done((bf16[128,2048]{1,0:T(8,128)(2,1)S(1)}, bf16[128,2048]{1,0:T(8,128)(2,1)S(1)}, u32[]{:S(2)}, u32[]{:S(2)}) %collective-permute-start.2) | collective-permute-done | bytes 524320 | tf_op jit(solution)/shard_map/ppermute | solution.py:18
  101.1 2.4 %gather_fusion.2 = bf16[288,2048]{1,0:T(8,128)(2,1)S(1)} fusion(bf16[128,2048]{1,0:T(8,128)(2,1)S(1)} %fusion.4, s32[1024]{0:T(1024)S(1)} %pad_clamp_fusion.1), kind=kCustom, calls=%fused_computation.2 | custom fusion | bytes 2360448 | tf_op jit(solution)/shard_map/gather | solution.py:61
  104.0 20.0 %all_to_all.21 = bf16[8,36,2048]{2,1,0:T(8,128)(2,1)S(1)} all-to-all(bf16[8,36,2048]{2,1,0:T(8,128)(2,1)S(1)} %broadcast_select_fusion), channel_id=1, replica_groups=mesh['section'=64,'expert'=8] {'expert'}, dimensions={0} | all-to-all | bytes 2359296 | tf_op jit(solution)/shard_map/all_to_all | solution.py:64
  124.2 3.8 %convolution_convert_fusion.1 = bf16[288,2048]{1,0:T(8,128)(2,1)S(1)} fusion(bf16[1,1,512,2048]{3,2,1,0:T(8,128)(2,1)} %param.9, bf16[288,2048]{1,0:T(8,128)(2,1)S(1)} %reshape.201, bf16[1,1,2048,512]{3,2,1,0:T(8,128)(2,1)} %param.8), kind=kOutput, calls=%fused_computation.9 | convolution fusion | flops 1209876480 | bytes 6553600 | tf_op jit(solution)/shard_map/dot_general | solution.py:25
  128.0 4.8 %convolution_convert_fusion = bf16[288,2048]{1,0:T(8,128)(2,1)} fusion(bf16[512,2048]{1,0:T(8,128)(2,1)} %collective-permute-done.1, bf16[288,2048]{1,0:T(8,128)(2,1)S(1)} %reshape.201, bf16[2048,512]{1,0:T(8,128)(2,1)} %collective-permute-done), kind=kOutput, calls=%fused_computation.8 | convolution fusion | flops 1209876480 | bytes 6553600 | tf_op jit(solution)/shard_map/dot_general | solution.py:25
  132.8 1.7 %add_convert_fusion = bf16[288,2048]{1,0:T(8,128)(2,1)S(1)} fusion(bf16[288,2048]{1,0:T(8,128)(2,1)} %convolution_convert_fusion, bf16[288,2048]{1,0:T(8,128)(2,1)S(1)} %convolution_convert_fusion.1), kind=kLoop, calls=%fused_computation.12 | loop fusion | flops 2359296 | bytes 3538944 | tf_op jit(solution)/shard_map/convert_element_type | solution.py:70
  134.5 1.2 reshape.202
  135.7 5.2 %all-to-all-start.3 = ((bf16[8,36,2048]{2,1,0:T(8,128)(2,1)}), bf16[8,36,2048]{2,1,0:T(8,128)(2,1)S(1)}, u32[]{:S(2)}, u32[]{:S(2)}) async-start(bf16[8,36,2048]{2,1,0:T(8,128)(2,1)} %reshape.202), calls=%async_computation.3 | async-start | bytes 2621440 | tf_op jit(solution)/shard_map/all_to_all | solution.py:71
  141.0 15.7 %all-to-all-done.3 = bf16[8,36,2048]{2,1,0:T(8,128)(2,1)S(1)} async-done(((bf16[8,36,2048]{2,1,0:T(8,128)(2,1)}), bf16[8,36,2048]{2,1,0:T(8,128)(2,1)S(1)}, u32[]{:S(2)}, u32[]{:S(2)}) %all-to-all-start.3) | async-done | bytes 1179680 | tf_op jit(solution)/shard_map/all_to_all | solution.py:71
  157.0 2.3 %gather_fusion.3 = bf16[256,2048]{1,0:T(8,128)(2,1)} fusion(bf16[288,2048]{1,0:T(8,128)(2,1)S(1)} %reshape.203, s32[1024]{0:T(1024)S(1)} %pad_clamp_fusion), kind=kCustom, calls=%fused_computation.3 | custom fusion | bytes 2098176 | tf_op jit(solution)/shard_map/gather | solution.py:74
  159.3 2.4 %reshape.205 = f32[128,2,2048]{2,1,0:T(2,128)S(1)} reshape(bf16[256,2048]{1,0:T(8,128)(2,1)} %gather_fusion.3) | data formatting | bytes 3145728 | tf_op jit(solution)/shard_map/convert_element_type | solution.py:74
  161.7 3.2 %multiply_reduce_fusion = f32[128,2048]{1,0:T(8,128)S(1)} fusion(f32[128,2,2048]{2,1,0:T(2,128)S(1)} %reshape.205, f32[128,2]{1,0:T(8,128)S(1)} %copy.15), kind=kLoop, calls=%fused_computation.14 | loop fusion | flops 786432 | bytes 3146752 | tf_op jit(solution)/shard_map/reduce_sum | solution.py:75
  164.9 0.9 fusion.5
  (67 shorter events, 8.4 us)
Async XLA Ops:
  0.0 45.3 %collective-permute-start.1 = (bf16[512,2048]{1,0:T(8,128)(2,1)}, bf16[512,2048]{1,0:T(8,128)(2,1)}, u32[]{:S(2)}, u32[]{:S(2)}) collective-permute-start(bf16[512,2048]{1,0:T(8,128)(2,1)} %bitcast.58), channel_id=1, source_target_pairs={{0,8},{8,0},{16,24},{24,16},{32,40},{40,32},{48,56},{56,48},{64,72... | collective-permute-start | bytes 6291464 | tf_op jit(solution)/shard_map/ppermute | solution.py:12
  1.9 43.4 %collective-permute-start = (bf16[2048,512]{1,0:T(8,128)(2,1)}, bf16[2048,512]{1,0:T(8,128)(2,1)}, u32[]{:S(2)}, u32[]{:S(2)}) collective-permute-start(bf16[2048,512]{1,0:T(8,128)(2,1)} %bitcast.59), channel_id=1, source_target_pairs={{0,8},{8,0},{16,24},{24,16},{32,40},{40,32},{48,56},{56,48},{64,72... | collective-permute-start | bytes 6291464 | tf_op jit(solution)/shard_map/ppermute | solution.py:12
  5.4 7.5 %copy-start.4 = (s32[256]{0:T(256)}, s32[256]{0:T(256)S(1)}, u32[]{:S(2)}) copy-start(s32[256]{0:T(256)S(1)} %and_select_fusion) | copy-start | bytes 3076
  13.3 0.6 copy-start.5
  41.1 4.2 %copy-start.1 = (bf16[288,2048]{1,0:T(8,128)(2,1)}, bf16[288,2048]{1,0:T(8,128)(2,1)S(1)}, u32[]{:S(2)}) copy-start(bf16[288,2048]{1,0:T(8,128)(2,1)S(1)} %reshape.195) | copy-start | bytes 3538948
  51.2 5.7 %copy-start.3 = (f32[2,128,2]{1,2,0:T(2,128)S(1)}, f32[2,128,2]{1,2,0:T(2,128)}, u32[]{:S(2)}) copy-start(f32[2,128,2]{1,2,0:T(2,128)} %param.7) | copy-start | bytes 6148
  51.2 21.8 %all-to-all-start.1 = ((bf16[8,36,2048]{2,1,0:T(8,128)(2,1)}), bf16[8,36,2048]{2,1,0:T(8,128)(2,1)S(1)}, u32[]{:S(2)}, u32[]{:S(2)}) async-start(bf16[8,36,2048]{2,1,0:T(8,128)(2,1)} %reshape.198), calls=%async_computation.1 | async-start | bytes 2621440 | tf_op jit(solution)/shard_map/all_to_all | solution.py:71
  74.6 1.4 copy-start.2
  76.0 3.2 %copy-start = (bf16[128,2048]{1,0:T(8,128)(2,1)S(1)}, bf16[128,2048]{1,0:T(8,128)(2,1)}, u32[]{:S(2)}) copy-start(bf16[128,2048]{1,0:T(8,128)(2,1)} %param.5) | copy-start | bytes 1572868
  79.3 21.4 %collective-permute-start.2 = (bf16[128,2048]{1,0:T(8,128)(2,1)S(1)}, bf16[128,2048]{1,0:T(8,128)(2,1)S(1)}, u32[]{:S(2)}, u32[]{:S(2)}) collective-permute-start(bf16[128,2048]{1,0:T(8,128)(2,1)S(1)} %fusion.2), channel_id=1, source_target_pairs={{0,16},{8,24},{16,32},{24,40},{32,48},{40,56},{48,64},{56,72},{64,... | collective-permute-start | bytes 1572872 | tf_op jit(solution)/shard_map/ppermute | solution.py:18
  135.7 21.0 %all-to-all-start.3 = ((bf16[8,36,2048]{2,1,0:T(8,128)(2,1)}), bf16[8,36,2048]{2,1,0:T(8,128)(2,1)S(1)}, u32[]{:S(2)}, u32[]{:S(2)}) async-start(bf16[8,36,2048]{2,1,0:T(8,128)(2,1)} %reshape.202), calls=%async_computation.3 | async-start | bytes 2621440 | tf_op jit(solution)/shard_map/all_to_all | solution.py:71
where the time goes:
time: 166 us
  waiting for transfers between devices  46 us (28%)
  blocking collectives  45.2 us (27%)
  local copies, waits for them, and re-layouts  25.7 us (15%)
  matrix products  16.9 us (10%)
  starting transfers between devices  16.8 us (10%)
  other arithmetic  14.9 us (9%)
    all_to_all x2, blocking collectives, body(): lax.all_to_all(outgoing, 'expert', split_axis=0, concat_axis=0, tiled=True)  45.2 us
    all_to_all x2, waiting for transfers between devices, body(): lax.all_to_all(expert_out, 'expert', split_axis=0, concat_axis=0, tiled=T...  29.8 us
    dot_general x4, matrix products, expert_half(): jnp.dot(hidden, down_part, preferred_element_type=jnp.float32)  16.9 us
    ppermute x1, waiting for transfers between devices, shifted(): return lax.ppermute(value, axis, pairs)  16.2 us
    all_to_all x2, starting transfers between devices, body(): lax.all_to_all(expert_out, 'expert', split_axis=0, concat_axis=0, tiled=T...  10.5 us
    reduce_sum x2, other arithmetic, body(): jnp.sum(gathered * share[:, :, None], axis=1)  6.33 us
    gather x4, local copies, waits for them, and re-layouts, body(): normed[anchor]  5.44 us
    ppermute x2, starting transfers between devices, swapped(): return lax.ppermute(value, axis, pairs)  4.32 us
  transfers between devices with their start and end apart: 5, of which 3 were waited for; matrix products, arithmetic and copies ran while one was open for 13% of the time, Pallas kernels for 0%

commit v1 on v0

v1 whole, which is shorter than its diff:
```python
import jax
import jax.numpy as jnp
from jax import lax
from jax.sharding import PartitionSpec as P

TICKS = 2


def swapped(value, axis, distance):
    mask = 2**distance
    pairs = [(source, source ^ mask) for source in range(lax.axis_size(axis))]
    return lax.ppermute(value, axis, pairs)


def shifted(value, axis, steps):
    count = lax.axis_size(axis)
    pairs = [(source, (source + steps) % count) for source in range(count)]
    return lax.ppermute(value, axis, pairs)


def expert_half(rows, up_part, down_part):
    hidden = jax.nn.gelu(
        jnp.einsum("gsd,dh->gsh", rows, up_part, preferred_element_type=jnp.float32),
        approximate=True,
    ).astype(jnp.bfloat16)
    return jnp.einsum(
        "gsh,hd->gsd", hidden, down_part, preferred_element_type=jnp.float32
    ).astype(jnp.bfloat16)


def slot_tables(ids, groups, slots):
    rows, top = ids.shape
    flat = ids.reshape(-1)
    count = rows * top
    chosen = (flat[:, None] == jnp.arange(groups, dtype=jnp.int32)[None, :]).astype(jnp.bfloat16)
    earlier = (
        jnp.arange(count, dtype=jnp.int32)[None, :] < jnp.arange(count, dtype=jnp.int32)[:, None]
    ).astype(jnp.bfloat16)
    before = jnp.dot(earlier, chosen, preferred_element_type=jnp.float32)
    position = jnp.sum(before * chosen.astype(jnp.float32), axis=1).astype(jnp.int32)
    position = position.reshape(rows, top)
    group_hit = ids.T[:, None, None, :] == jnp.arange(groups, dtype=jnp.int32)[None, :, None, None]
    slot_hit = position.T[:, None, None, :] == jnp.arange(slots, dtype=jnp.int32)[None, None, :, None]
    return (group_hit & slot_hit).astype(jnp.bfloat16)


def body(tokens, routes, combine, up_weight, down_weight):
    rows = tokens.shape[0]
    top = routes.shape[2]
    groups = lax.axis_size("expert")
    slots = min(rows, rows * top * 9 // (8 * groups))
    up_local = up_weight.reshape(up_weight.shape[2], up_weight.shape[3])
    down_local = down_weight.reshape(down_weight.shape[2], down_weight.shape[3])
    partner_up, partner_down = swapped((up_local, down_local), "section", 0)
    state = tokens
    for tick in range(TICKS):
        if tick > 0:
            state = shifted(state, "section", 2)
        weights = combine[tick]
        select = slot_tables(routes[tick], groups, slots)
        state_f = state.astype(jnp.float32)
        normed = (
            state_f * lax.rsqrt(jnp.mean(state_f * state_f, axis=1, keepdims=True) + 1e-06)
        ).astype(jnp.bfloat16)
        share = weights / jnp.sum(weights, axis=1, keepdims=True)
        dispatch = jnp.sum(select, axis=0)
        outgoing = jnp.einsum(
            "gsr,rd->gsd", dispatch, normed, preferred_element_type=jnp.float32
        ).astype(jnp.bfloat16)
        received = lax.all_to_all(outgoing, "expert", split_axis=0, concat_axis=0, tiled=True)
        own_part = lax.optimization_barrier(expert_half(received, up_local, down_local))
        other_part = lax.optimization_barrier(expert_half(received, partner_up, partner_down))
        summed = own_part.astype(jnp.float32) + other_part.astype(jnp.float32)
        expert_out = summed.astype(jnp.bfloat16)
        answers = lax.all_to_all(expert_out, "expert", split_axis=0, concat_axis=0, tiled=True)
        total = state_f
        for k in range(top):
            picked = jnp.einsum(
                "gsr,gsd->rd", select[k], answers, preferred_element_type=jnp.float32
            )
            total = total + share[:, k : k + 1] * picked
        state = total.astype(jnp.bfloat16)
    return state


def solution(mesh):
    in_specs = (
        P(("section", "expert"), None),
        P(None, ("section", "expert"), None),
        P(None, ("section", "expert"), None),
        P("section", "expert", None, None),
        P("section", "expert", None, None),
    )
    out_specs = P(("section", "expert"), None)
    return jax.shard_map(body, mesh=mesh, in_specs=in_specs, out_specs=out_specs, check_vma=False)
```

time: 166 us -> 145 us (0.87)
  the two profiles are of different devices: /device:TPU:2 before, /device:TPU:8 now
where the time goes in v1:
time: 145 us
  waiting for transfers between devices  49.7 us (34%)
  blocking collectives  48.2 us (33%)
  matrix products  22.6 us (16%)
  starting transfers between devices  15.1 us (10%)
  other arithmetic  7.22 us (5%)
  local copies, waits for them, and re-layouts  1.6 us (1%)
    all_to_all x2, blocking collectives, body(): lax.all_to_all(outgoing, 'expert', split_axis=0, concat_axis=0, tiled=True)  48.2 us
    all_to_all x2, waiting for transfers between devices, body(): lax.all_to_all(expert_out, 'expert', split_axis=0, concat_axis=0, tiled=T...  31.6 us
    dot_general x4, matrix products, expert_half(): jnp.einsum('gsh,hd->gsd', hidden, down_part, preferred_element_type=jnp.f...  18.2 us
    ppermute x1, waiting for transfers between devices, shifted(): return lax.ppermute(value, axis, pairs)  18.1 us
    all_to_all x2, starting transfers between devices, body(): lax.all_to_all(expert_out, 'expert', split_axis=0, concat_axis=0, tiled=T...  8.73 us
    convert_element_type x2, other arithmetic, body(): expert_out = summed.astype(jnp.bfloat16)  5.52 us
    ppermute x2, starting transfers between devices, swapped(): return lax.ppermute(value, axis, pairs)  4.45 us
  transfers between devices with their start and end apart: 5, of which 3 were waited for; matrix products, arithmetic and copies ran while one was open for 6% of the time, Pallas kernels for 0%

profile of v1, /device:TPU:8, one launch (start us, length us, event | category | flops | bytes accessed | tf_op | source)
XLA Modules:
  0.0 144.6 jit_solution(13098611268886158409)
XLA Ops:
  0.0 2.0 %collective-permute-start.1 = (bf16[512,2048]{1,0:T(8,128)(2,1)}, bf16[512,2048]{1,0:T(8,128)(2,1)}, u32[]{:S(2)}, u32[]{:S(2)}) collective-permute-start(bf16[512,2048]{1,0:T(8,128)(2,1)} %bitcast.128), channel_id=1, source_target_pairs={{0,8},{8,0},{16,24},{24,16},{32,40},{40,32},{48,56},{56,48},{64,72... | collective-permute-start | bytes 6291464 | tf_op jit(solution)/shard_map/ppermute | solution.py:12
  2.1 2.4 %collective-permute-start = (bf16[2048,512]{1,0:T(8,128)(2,1)}, bf16[2048,512]{1,0:T(8,128)(2,1)}, u32[]{:S(2)}, u32[]{:S(2)}) collective-permute-start(bf16[2048,512]{1,0:T(8,128)(2,1)} %bitcast.129), channel_id=1, source_target_pairs={{0,8},{8,0},{16,24},{24,16},{32,40},{40,32},{48,56},{56,48},{64,72... | collective-permute-start | bytes 6291464 | tf_op jit(solution)/shard_map/ppermute | solution.py:12
  4.5 0.7 slice_bitcast_fusion.13
  5.2 0.1 copy.6
  5.3 0.1 eq.105
  5.4 0.2 fusion.22
  5.6 0.1 convert_element_type.108
  5.9 1.2 fusion.24
  7.2 0.6 convolution_convert_fusion.1
  7.8 26.0 %all_to_all.20 = bf16[8,36,2048]{2,1,0:T(8,128)(2,1)S(1)} all-to-all(bf16[8,36,2048]{2,1,0:T(8,128)(2,1)S(1)} %convolution_convert_fusion.1), channel_id=1, replica_groups=mesh['section'=64,'expert'=8] {'expert'}, dimensions={0} | all-to-all | bytes 2359296 | tf_op jit(solution)/shard_map/all_to_all | solution.py:70
  33.8 4.0 %convolution_convert_fusion.5 = bf16[8,36,2048]{2,1,0:T(8,128)(2,1)S(1)} fusion(bf16[1,1,512,2048]{3,2,1,0:T(8,128)(2,1)} %param.9, bf16[8,36,2048]{2,1,0:T(8,128)(2,1)S(1)} %all_to_all.20, bf16[1,1,2048,512]{3,2,1,0:T(8,128)(2,1)} %param.8), kind=kOutput, calls=%fused_computation.5 | convolution fusion | flops 1209876480 | bytes 6553600 | tf_op jit(solution)/shard_map/gsh,hd->gsd/dot_general | solution.py:26
  37.8 5.1 %convolution_convert_fusion.4 = bf16[8,36,2048]{2,1,0:T(8,128)(2,1)} fusion(bf16[512,2048]{1,0:T(8,128)(2,1)} %collective-permute-done.1, bf16[8,36,2048]{2,1,0:T(8,128)(2,1)S(1)} %all_to_all.20, bf16[2048,512]{1,0:T(8,128)(2,1)} %collective-permute-done), kind=kOutput, calls=%fused_computation.4 | convolution fusion | flops 1209876480 | bytes 6553600 | tf_op jit(solution)/shard_map/gsh,hd->gsd/dot_general | solution.py:26
  42.9 2.8 %add_convert_fusion.1 = bf16[8,36,2048]{2,1,0:T(8,128)(2,1)} fusion(bf16[8,36,2048]{2,1,0:T(8,128)(2,1)} %convolution_convert_fusion.4, bf16[8,36,2048]{2,1,0:T(8,128)(2,1)S(1)} %convolution_convert_fusion.5), kind=kLoop, calls=%fused_computation.7 | loop fusion | flops 2359296 | bytes 3538944 | tf_op jit(solution)/shard_map/convert_element_type | solution.py:74
  45.7 4.4 %all-to-all-start.1 = ((bf16[8,36,2048]{2,1,0:T(8,128)(2,1)}), bf16[8,36,2048]{2,1,0:T(8,128)(2,1)S(1)}, u32[]{:S(2)}, u32[]{:S(2)}) async-start(bf16[8,36,2048]{2,1,0:T(8,128)(2,1)} %add_convert_fusion.1), calls=%async_computation.1 | async-start | bytes 2621440 | tf_op jit(solution)/shard_map/all_to_all | solution.py:75
  50.2 0.1 eq.115
  50.4 0.2 fusion.23
  50.6 0.1 convert_element_type.124
  50.9 15.7 %all-to-all-done.1 = bf16[8,36,2048]{2,1,0:T(8,128)(2,1)S(1)} async-done(((bf16[8,36,2048]{2,1,0:T(8,128)(2,1)}), bf16[8,36,2048]{2,1,0:T(8,128)(2,1)S(1)}, u32[]{:S(2)}, u32[]{:S(2)}) %all-to-all-start.1) | async-done | bytes 1179680 | tf_op jit(solution)/shard_map/all_to_all | solution.py:75
  66.6 0.5 fusion.7
  67.1 0.5 fusion.8
  67.6 1.9 %collective-permute-start.2 = (bf16[128,2048]{1,0:T(8,128)(2,1)S(1)}, bf16[128,2048]{1,0:T(8,128)(2,1)S(1)}, u32[]{:S(2)}, u32[]{:S(2)}) collective-permute-start(bf16[128,2048]{1,0:T(8,128)(2,1)S(1)} %fusion.8), channel_id=1, source_target_pairs={{0,16},{8,24},{16,32},{24,40},{32,48},{40,56},{48,64},{56,72},{64,... | collective-permute-start | bytes 1572872 | tf_op jit(solution)/shard_map/ppermute | solution.py:18
  69.6 18.1 %collective-permute-done.2 = bf16[128,2048]{1,0:T(8,128)(2,1)S(1)} collective-permute-done((bf16[128,2048]{1,0:T(8,128)(2,1)S(1)}, bf16[128,2048]{1,0:T(8,128)(2,1)S(1)}, u32[]{:S(2)}, u32[]{:S(2)}) %collective-permute-start.2) | collective-permute-done | bytes 524320 | tf_op jit(solution)/shard_map/ppermute | solution.py:18
  87.7 0.2 fusion.26
  87.9 0.6 convolution_convert_fusion
  88.5 22.2 %all_to_all.21 = bf16[8,36,2048]{2,1,0:T(8,128)(2,1)S(1)} all-to-all(bf16[8,36,2048]{2,1,0:T(8,128)(2,1)S(1)} %convolution_convert_fusion), channel_id=1, replica_groups=mesh['section'=64,'expert'=8] {'expert'}, dimensions={0} | all-to-all | bytes 2359296 | tf_op jit(solution)/shard_map/all_to_all | solution.py:70
  110.6 4.0 %convolution_convert_fusion.2 = bf16[8,36,2048]{2,1,0:T(8,128)(2,1)S(1)} fusion(bf16[512,2048]{1,0:T(8,128)(2,1)} %collective-permute-done.1, bf16[8,36,2048]{2,1,0:T(8,128)(2,1)S(1)} %all_to_all.21, bf16[2048,512]{1,0:T(8,128)(2,1)} %collective-permute-done), kind=kOutput, calls=%fused_computation.2 | convolution fusion | flops 1209876480 | bytes 6553600 | tf_op jit(solution)/shard_map/gsh,hd->gsd/dot_general | solution.py:26
  114.7 5.1 %convolution_convert_fusion.3 = bf16[8,36,2048]{2,1,0:T(8,128)(2,1)} fusion(bf16[1,1,512,2048]{3,2,1,0:T(8,128)(2,1)} %param.9, bf16[8,36,2048]{2,1,0:T(8,128)(2,1)S(1)} %all_to_all.21, bf16[1,1,2048,512]{3,2,1,0:T(8,128)(2,1)} %param.8), kind=kOutput, calls=%fused_computation.3 | convolution fusion | flops 1209876480 | bytes 6553600 | tf_op jit(solution)/shard_map/gsh,hd->gsd/dot_general | solution.py:26
  119.8 2.8 %add_convert_fusion = bf16[8,36,2048]{2,1,0:T(8,128)(2,1)} fusion(bf16[8,36,2048]{2,1,0:T(8,128)(2,1)S(1)} %convolution_convert_fusion.2, bf16[8,36,2048]{2,1,0:T(8,128)(2,1)} %convolution_convert_fusion.3), kind=kLoop, calls=%fused_computation.6 | loop fusion | flops 2359296 | bytes 3538944 | tf_op jit(solution)/shard_map/convert_element_type | solution.py:74
  122.5 4.3 %all-to-all-start.3 = ((bf16[8,36,2048]{2,1,0:T(8,128)(2,1)}), bf16[8,36,2048]{2,1,0:T(8,128)(2,1)S(1)}, u32[]{:S(2)}, u32[]{:S(2)}) async-start(bf16[8,36,2048]{2,1,0:T(8,128)(2,1)} %add_convert_fusion), calls=%async_computation.3 | async-start | bytes 2621440 | tf_op jit(solution)/shard_map/all_to_all | solution.py:75
  126.9 15.9 %all-to-all-done.3 = bf16[8,36,2048]{2,1,0:T(8,128)(2,1)S(1)} async-done(((bf16[8,36,2048]{2,1,0:T(8,128)(2,1)}), bf16[8,36,2048]{2,1,0:T(8,128)(2,1)S(1)}, u32[]{:S(2)}, u32[]{:S(2)}) %all-to-all-start.3) | async-done | bytes 1179680 | tf_op jit(solution)/shard_map/all_to_all | solution.py:75
  142.8 0.5 fusion
  143.3 1.3 fusion.9
  (25 shorter events, 0.5 us)
Async XLA Ops:
  0.0 7.2 %copy-start = (bf16[128,2048]{1,0:T(8,128)(2,1)S(1)}, bf16[128,2048]{1,0:T(8,128)(2,1)}, u32[]{:S(2)}) copy-start(bf16[128,2048]{1,0:T(8,128)(2,1)} %param.5) | copy-start | bytes 1572868
  0.0 37.8 %collective-permute-start.1 = (bf16[512,2048]{1,0:T(8,128)(2,1)}, bf16[512,2048]{1,0:T(8,128)(2,1)}, u32[]{:S(2)}, u32[]{:S(2)}) collective-permute-start(bf16[512,2048]{1,0:T(8,128)(2,1)} %bitcast.128), channel_id=1, source_target_pairs={{0,8},{8,0},{16,24},{24,16},{32,40},{40,32},{48,56},{56,48},{64,72... | collective-permute-start | bytes 6291464 | tf_op jit(solution)/shard_map/ppermute | solution.py:12
  2.1 35.8 %collective-permute-start = (bf16[2048,512]{1,0:T(8,128)(2,1)}, bf16[2048,512]{1,0:T(8,128)(2,1)}, u32[]{:S(2)}, u32[]{:S(2)}) collective-permute-start(bf16[2048,512]{1,0:T(8,128)(2,1)} %bitcast.129), channel_id=1, source_target_pairs={{0,8},{8,0},{16,24},{24,16},{32,40},{40,32},{48,56},{56,48},{64,72... | collective-permute-start | bytes 6291464 | tf_op jit(solution)/shard_map/ppermute | solution.py:12
  45.7 5.1 %copy-start.1 = (f32[2,128,2]{1,2,0:T(2,128)S(1)}, f32[2,128,2]{1,2,0:T(2,128)}, u32[]{:S(2)}) copy-start(f32[2,128,2]{1,2,0:T(2,128)} %param.7) | copy-start | bytes 6148
  45.7 20.9 %all-to-all-start.1 = ((bf16[8,36,2048]{2,1,0:T(8,128)(2,1)}), bf16[8,36,2048]{2,1,0:T(8,128)(2,1)S(1)}, u32[]{:S(2)}, u32[]{:S(2)}) async-start(bf16[8,36,2048]{2,1,0:T(8,128)(2,1)} %add_convert_fusion.1), calls=%async_computation.1 | async-start | bytes 2621440 | tf_op jit(solution)/shard_map/all_to_all | solution.py:75
  67.6 20.1 %collective-permute-start.2 = (bf16[128,2048]{1,0:T(8,128)(2,1)S(1)}, bf16[128,2048]{1,0:T(8,128)(2,1)S(1)}, u32[]{:S(2)}, u32[]{:S(2)}) collective-permute-start(bf16[128,2048]{1,0:T(8,128)(2,1)S(1)} %fusion.8), channel_id=1, source_target_pairs={{0,16},{8,24},{16,32},{24,40},{32,48},{40,56},{48,64},{56,72},{64,... | collective-permute-start | bytes 1572872 | tf_op jit(solution)/shard_map/ppermute | solution.py:18
  122.5 20.2 %all-to-all-start.3 = ((bf16[8,36,2048]{2,1,0:T(8,128)(2,1)}), bf16[8,36,2048]{2,1,0:T(8,128)(2,1)S(1)}, u32[]{:S(2)}, u32[]{:S(2)}) async-start(bf16[8,36,2048]{2,1,0:T(8,128)(2,1)} %add_convert_fusion), calls=%async_computation.3 | async-start | bytes 2621440 | tf_op jit(solution)/shard_map/all_to_all | solution.py:75

commit v2 on v1

--- a/solution.py
+++ b/solution.py
@@ -1,6 +1,8 @@
 import jax
 import jax.numpy as jnp
 from jax import lax
+from jax.experimental import pallas as pl
+from jax.experimental.pallas import tpu as pltpu
 from jax.sharding import PartitionSpec as P
 
 TICKS = 2
@@ -18,14 +20,83 @@
     return lax.ppermute(value, axis, pairs)
 
 
-def expert_half(rows, up_part, down_part):
-    hidden = jax.nn.gelu(
-        jnp.einsum("gsd,dh->gsh", rows, up_part, preferred_element_type=jnp.float32),
-        approximate=True,
-    ).astype(jnp.bfloat16)
-    return jnp.einsum(
-        "gsh,hd->gsd", hidden, down_part, preferred_element_type=jnp.float32
-    ).astype(jnp.bfloat16)
+def expert_kernel(x_ref, own_up, own_down, far_up, far_down, out_ref, half_acc, sum_acc):
+    step = pl.program_id(0)
+    chunks = pl.num_programs(0) // 2
+    half = step // chunks
+    chunk = step % chunks
+
+    def partial(up_ref, down_ref):
+        hidden = jax.nn.gelu(
+            jnp.dot(x_ref[...], up_ref[...], preferred_element_type=jnp.float32), approximate=True
+        ).astype(jnp.bfloat16)
+        return jnp.dot(hidden, down_ref[...], preferred_element_type=jnp.float32)
+
+    def accumulate(value):
+        @pl.when(chunk == 0)
+        def _():
+            half_acc[...] = value
+
+        @pl.when(chunk > 0)
+        def _():
+            half_acc[...] += value
+
+    @pl.when(half == 0)
+    def _():
+        accumulate(partial(own_up, own_down))
+
+    @pl.when(half == 1)
+    def _():
+        accumulate(partial(far_up, far_down))
+
+    @pl.when((chunk == chunks - 1) & (half == 0))
+    def _():
+        sum_acc[...] = half_acc[...].astype(jnp.bfloat16).astype(jnp.float32)
+
+    @pl.when((chunk == chunks - 1) & (half == 1))
+    def _():
+        total = sum_acc[...] + half_acc[...].astype(jnp.bfloat16).astype(jnp.float32)
+        out_ref[...] = total.astype(out_ref.dtype)
+
+
+def expert_full(rows, own_up, own_down, far_up, far_down, chunk=256):
+    count, width = rows.shape
+    hidden = own_up.shape[1]
+    chunks = hidden // chunk
+    last = chunks - 1
+
+    def own_col(i):
+        return jnp.minimum(i, last)
+
+    def far_col(i):
+        return jnp.maximum(i - chunks, 0)
+
+    cost = pl.CostEstimate(
+        flops=2 * 2 * count * width * hidden * 2,
+        transcendentals=count * hidden * 2,
+        bytes_accessed=4 * width * hidden * 2 + 2 * count * width * 2,
+    )
+    return pl.pallas_call(
+        expert_kernel,
+        grid=(2 * chunks,),
+        in_specs=[
+            pl.BlockSpec((count, width), lambda i: (0, 0)),
+            pl.BlockSpec((width, chunk), lambda i: (0, own_col(i))),
+            pl.BlockSpec((chunk, width), lambda i: (own_col(i), 0)),
+            pl.BlockSpec((width, chunk), lambda i: (0, far_col(i))),
+            pl.BlockSpec((chunk, width), lambda i: (far_col(i), 0)),
+        ],
+        out_specs=pl.BlockSpec((count, width), lambda i: (0, 0)),
+        out_shape=jax.ShapeDtypeStruct((count, width), jnp.bfloat16),
+        scratch_shapes=[
+            pltpu.VMEM((count, width), jnp.float32),
+            pltpu.VMEM((count, width), jnp.float32),
+        ],
+        compiler_params=pltpu.CompilerParams(
+            dimension_semantics=("arbitrary",), vmem_limit_bytes=48 * 1024 * 1024
+        ),
+        cost_estimate=cost,
+    )(rows, own_up, own_down, far_up, far_down)
 
 
 def slot_tables(ids, groups, slots):
@@ -49,6 +120,7 @@
     top = routes.shape[2]
     groups = lax.axis_size("expert")
     slots = min(rows, rows * top * 9 // (8 * groups))
+    slots = -(-slots // 8) * 8
     up_local = up_weight.reshape(up_weight.shape[2], up_weight.shape[3])
     down_local = down_weight.reshape(down_weight.shape[2], down_weight.shape[3])
     partner_up, partner_down = swapped((up_local, down_local), "section", 0)
@@ -68,10 +140,9 @@
             "gsr,rd->gsd", dispatch, normed, preferred_element_type=jnp.float32
         ).astype(jnp.bfloat16)
         received = lax.all_to_all(outgoing, "expert", split_axis=0, concat_axis=0, tiled=True)
-        own_part = lax.optimization_barrier(expert_half(received, up_local, down_local))
-        other_part = lax.optimization_barrier(expert_half(received, partner_up, partner_down))
-        summed = own_part.astype(jnp.float32) + other_part.astype(jnp.float32)
-        expert_out = summed.astype(jnp.bfloat16)
+        expert_out = expert_full(
+            received.reshape(groups * slots, -1), up_local, down_local, partner_up, partner_down
+        ).reshape(groups, slots, -1)
         answers = lax.all_to_all(expert_out, "expert", split_axis=0, concat_axis=0, tiled=True)
         total = state_f
         for k in range(top):

time: 145 us -> 144 us (level)
  Pallas kernels: 0 us -> 21.2 us
  matrix products: 22.6 us -> 5.34 us
  other arithmetic: 7.22 us -> 1.69 us
    pallas_call x0 -> x2, Pallas kernels: none -> 21.2 us  [expert_full(): pl.pallas_call(expert_kernel, grid=(2 * chunks,), in_specs=[pl.BlockSpec(...]
    dot_general x4 -> x0, matrix products: 18.2 us -> none  [expert_half(): jnp.einsum('gsh,hd->gsd', hidden, down_part, preferred_element_type=jnp.f...]
    convert_element_type x2 -> x0, other arithmetic: 5.52 us -> none  [body(): expert_out = summed.astype(jnp.bfloat16)]
  transfers between devices with their start and end apart: 5 -> 5, of which waited for: 3 -> 3; matrix products, arithmetic and copies ran while one was open for 6% -> 3% of each run, Pallas kernels for 0% -> 0%
where the time goes in v2:
time: 144 us; the launch traced here: 143 us
  waiting for transfers between devices  49.7 us (35%)
  blocking collectives  48.3 us (34%)
  Pallas kernels  21.2 us (15%)
  starting transfers between devices  15.1 us (10%)
  matrix products  5.34 us (4%)
  other arithmetic  1.69 us (1%)
  local copies, waits for them, and re-layouts  1.61 us (1%)
    all_to_all x2, blocking collectives, body(): lax.all_to_all(outgoing, 'expert', split_axis=0, concat_axis=0, tiled=True)  48.3 us
    all_to_all x2, waiting for transfers between devices, body(): lax.all_to_all(expert_out, 'expert', split_axis=0, concat_axis=0, tiled=T...  31.6 us
    pallas_call x2, Pallas kernels, expert_full(): pl.pallas_call(expert_kernel, grid=(2 * chunks,), in_specs=[pl.BlockSpec(...  21.2 us
    ppermute x1, waiting for transfers between devices, shifted(): return lax.ppermute(value, axis, pairs)  18.1 us
    all_to_all x2, starting transfers between devices, body(): lax.all_to_all(expert_out, 'expert', split_axis=0, concat_axis=0, tiled=T...  8.71 us
    ppermute x2, starting transfers between devices, swapped(): return lax.ppermute(value, axis, pairs)  4.45 us
    dot_general x4, matrix products, body(): jnp.einsum('gsr,gsd->rd', select[k], answers, preferred_element_type=jnp....  3.8 us
  transfers between devices with their start and end apart: 5, of which 3 were waited for; matrix products, arithmetic and copies ran while one was open for 3% of the time, Pallas kernels for 0%

profile of v2, /device:TPU:8, one launch (start us, length us, event | category | flops | bytes accessed | tf_op | source)
XLA Modules:
  0.0 143.2 jit_solution(12648637082972294458)
XLA Ops:
  0.0 2.0 %collective-permute-start = (bf16[2048,512]{1,0:T(8,128)(2,1)}, bf16[2048,512]{1,0:T(8,128)(2,1)}, u32[]{:S(2)}, u32[]{:S(2)}) collective-permute-start(bf16[2048,512]{1,0:T(8,128)(2,1)} %bitcast.80), channel_id=1, source_target_pairs={{0,8},{8,0},{16,24},{24,16},{32,40},{40,32},{48,56},{56,48},{64,72... | collective-permute-start | bytes 6291464 | tf_op jit(solution)/shard_map/ppermute | solution.py:14
  2.1 2.4 %collective-permute-start.1 = (bf16[512,2048]{1,0:T(8,128)(2,1)}, bf16[512,2048]{1,0:T(8,128)(2,1)}, u32[]{:S(2)}, u32[]{:S(2)}) collective-permute-start(bf16[512,2048]{1,0:T(8,128)(2,1)} %bitcast.85), channel_id=1, source_target_pairs={{0,8},{8,0},{16,24},{24,16},{32,40},{40,32},{48,56},{56,48},{64,72... | collective-permute-start | bytes 6291464 | tf_op jit(solution)/shard_map/ppermute | solution.py:14
  4.5 0.7 slice_bitcast_fusion.13
  5.2 0.1 copy.6
  5.3 0.1 eq.105
  5.4 0.2 fusion.10
  5.6 0.1 convert_element_type.66
  5.8 0.1 copy.7
  5.9 1.2 fusion.12
  7.2 0.6 convolution_convert_fusion.1
  7.8 0.0 copy-start
  7.8 26.2 %all_to_all.20 = bf16[8,40,2048]{2,1,0:T(8,128)(2,1)S(1)} all-to-all(bf16[8,40,2048]{2,1,0:T(8,128)(2,1)S(1)} %convolution_convert_fusion.1), channel_id=1, replica_groups=mesh['section'=64,'expert'=8] {'expert'}, dimensions={0} | all-to-all | bytes 2621440 | tf_op jit(solution)/shard_map/all_to_all | solution.py:142
  33.9 10.6 %shard_map.55 = bf16[320,2048]{1,0:T(8,128)(2,1)} custom-call(bf16[320,2048]{1,0:T(8,128)(2,1)S(1)} %bitcast.83, bf16[2048,512]{1,0:T(8,128)(2,1)S(1)} %bitcast.81, bf16[512,2048]{1,0:T(8,128)(2,1)} %bitcast.86, bf16[2048,512]{1,0:T(8,128)(2,1)} %collective-permute-done.far_up, bf16[512,2048]{1,0:T(8,128)(2,1)} %collective-permute-done.1.far_down), custom_call_target="tpu_custom_call" | custom-call | flops 2684354560 | bytes 11010048 | tf_op jit(solution)/shard_map/pallas_call | solution.py:79
  44.6 4.4 %all-to-all-start.1 = ((bf16[8,40,2048]{2,1,0:T(8,128)(2,1)}), bf16[8,40,2048]{2,1,0:T(8,128)(2,1)S(1)}, u32[]{:S(2)}, u32[]{:S(2)}) async-start(bf16[8,40,2048]{2,1,0:T(8,128)(2,1)} %bitcast.10), calls=%async_computation.1 | async-start | bytes 2621440 | tf_op jit(solution)/shard_map/all_to_all | solution.py:146
  49.0 0.1 copy.8
  49.1 0.1 eq.115
  49.2 0.2 fusion.11
  49.5 0.1 convert_element_type.75
  49.6 0.1 copy.9
  49.8 15.7 %all-to-all-done.1 = bf16[8,40,2048]{2,1,0:T(8,128)(2,1)S(1)} async-done(((bf16[8,40,2048]{2,1,0:T(8,128)(2,1)}), bf16[8,40,2048]{2,1,0:T(8,128)(2,1)S(1)}, u32[]{:S(2)}, u32[]{:S(2)}) %all-to-all-start.1) | async-done | bytes 1310752 | tf_op jit(solution)/shard_map/all_to_all | solution.py:146
  65.5 1.5 %fusion.7 = f32[128,2048]{1,0:T(8,128)S(1)} fusion(bf16[8,40,2048]{2,1,0:T(8,128)(2,1)S(1)} %all-to-all-done.1, bf16[128,2048]{1,0:T(8,128)(2,1)} %param.5, f32[128]{0:T(128)S(1)} %get-tuple-element.16, pred[2,8,40,128]{3,2,1,0:T(8,128)(4,1)S(1)} %broadcast_and_fusion.1), kind=kOutput, calls=%fused_computation.13 | convolution fusion | flops 168558592 | bytes 2925056 | tf_op jit(solution)/shard_map/gsr,gsd->rd/dot_general | solution.py:149
  67.0 0.5 fusion.8
  67.5 1.9 %collective-permute-start.2 = (bf16[128,2048]{1,0:T(8,128)(2,1)S(1)}, bf16[128,2048]{1,0:T(8,128)(2,1)S(1)}, u32[]{:S(2)}, u32[]{:S(2)}) collective-permute-start(bf16[128,2048]{1,0:T(8,128)(2,1)S(1)} %fusion.8), channel_id=1, source_target_pairs={{0,16},{8,24},{16,32},{24,40},{32,48},{40,56},{48,64},{56,72},{64,... | collective-permute-start | bytes 1572872 | tf_op jit(solution)/shard_map/ppermute | solution.py:20
  69.5 18.1 %collective-permute-done.2 = bf16[128,2048]{1,0:T(8,128)(2,1)S(1)} collective-permute-done((bf16[128,2048]{1,0:T(8,128)(2,1)S(1)}, bf16[128,2048]{1,0:T(8,128)(2,1)S(1)}, u32[]{:S(2)}, u32[]{:S(2)}) %collective-permute-start.2) | collective-permute-done | bytes 524320 | tf_op jit(solution)/shard_map/ppermute | solution.py:20
  87.6 0.2 fusion.14
  87.8 0.6 convolution_convert_fusion
  88.4 22.2 %all_to_all.21 = bf16[8,40,2048]{2,1,0:T(8,128)(2,1)S(1)} all-to-all(bf16[8,40,2048]{2,1,0:T(8,128)(2,1)S(1)} %convolution_convert_fusion), channel_id=1, replica_groups=mesh['section'=64,'expert'=8] {'expert'}, dimensions={0} | all-to-all | bytes 2621440 | tf_op jit(solution)/shard_map/all_to_all | solution.py:142
  110.5 10.6 %shard_map.56 = bf16[320,2048]{1,0:T(8,128)(2,1)} custom-call(bf16[320,2048]{1,0:T(8,128)(2,1)S(1)} %bitcast.84, bf16[2048,512]{1,0:T(8,128)(2,1)S(1)} %bitcast.82, bf16[512,2048]{1,0:T(8,128)(2,1)} %bitcast.87, bf16[2048,512]{1,0:T(8,128)(2,1)} %collective-permute-done.far_up, bf16[512,2048]{1,0:T(8,128)(2,1)} %collective-permute-done.1.far_down), custom_call_target="tpu_custom_call" | custom-call | flops 2684354560 | bytes 11010048 | tf_op jit(solution)/shard_map/pallas_call | solution.py:79
  121.2 4.3 %all-to-all-start.3 = ((bf16[8,40,2048]{2,1,0:T(8,128)(2,1)}), bf16[8,40,2048]{2,1,0:T(8,128)(2,1)S(1)}, u32[]{:S(2)}, u32[]{:S(2)}) async-start(bf16[8,40,2048]{2,1,0:T(8,128)(2,1)} %bitcast.23), calls=%async_computation.3 | async-start | bytes 2621440 | tf_op jit(solution)/shard_map/all_to_all | solution.py:146
  125.5 15.9 %all-to-all-done.3 = bf16[8,40,2048]{2,1,0:T(8,128)(2,1)S(1)} async-done(((bf16[8,40,2048]{2,1,0:T(8,128)(2,1)}), bf16[8,40,2048]{2,1,0:T(8,128)(2,1)S(1)}, u32[]{:S(2)}, u32[]{:S(2)}) %all-to-all-start.3) | async-done | bytes 1310752 | tf_op jit(solution)/shard_map/all_to_all | solution.py:146
  141.4 0.5 fusion
  141.9 1.3 fusion.9
  (23 shorter events, 0.3 us)
Async XLA Ops:
  0.0 7.2 %copy-start.1 = (bf16[128,2048]{1,0:T(8,128)(2,1)S(1)}, bf16[128,2048]{1,0:T(8,128)(2,1)}, u32[]{:S(2)}) copy-start(bf16[128,2048]{1,0:T(8,128)(2,1)} %param.5) | copy-start | bytes 1572868
  0.0 33.9 %collective-permute-start = (bf16[2048,512]{1,0:T(8,128)(2,1)}, bf16[2048,512]{1,0:T(8,128)(2,1)}, u32[]{:S(2)}, u32[]{:S(2)}) collective-permute-start(bf16[2048,512]{1,0:T(8,128)(2,1)} %bitcast.80), channel_id=1, source_target_pairs={{0,8},{8,0},{16,24},{24,16},{32,40},{40,32},{48,56},{56,48},{64,72... | collective-permute-start | bytes 6291464 | tf_op jit(solution)/shard_map/ppermute | solution.py:14
  2.1 31.9 %collective-permute-start.1 = (bf16[512,2048]{1,0:T(8,128)(2,1)}, bf16[512,2048]{1,0:T(8,128)(2,1)}, u32[]{:S(2)}, u32[]{:S(2)}) collective-permute-start(bf16[512,2048]{1,0:T(8,128)(2,1)} %bitcast.85), channel_id=1, source_target_pairs={{0,8},{8,0},{16,24},{24,16},{32,40},{40,32},{48,56},{56,48},{64,72... | collective-permute-start | bytes 6291464 | tf_op jit(solution)/shard_map/ppermute | solution.py:14
  7.8 26.2 %copy-start = (bf16[1,1,2048,512]{3,2,1,0:T(8,128)(2,1)S(1)}, bf16[1,1,2048,512]{3,2,1,0:T(8,128)(2,1)}, u32[]{:S(2)}) copy-start(bf16[1,1,2048,512]{3,2,1,0:T(8,128)(2,1)} %param.8) | copy-start | bytes 6291460
  44.6 5.1 %copy-start.2 = (f32[2,128,2]{1,2,0:T(2,128)S(1)}, f32[2,128,2]{1,2,0:T(2,128)}, u32[]{:S(2)}) copy-start(f32[2,128,2]{1,2,0:T(2,128)} %param.7) | copy-start | bytes 6148
  44.6 20.9 %all-to-all-start.1 = ((bf16[8,40,2048]{2,1,0:T(8,128)(2,1)}), bf16[8,40,2048]{2,1,0:T(8,128)(2,1)S(1)}, u32[]{:S(2)}, u32[]{:S(2)}) async-start(bf16[8,40,2048]{2,1,0:T(8,128)(2,1)} %bitcast.10), calls=%async_computation.1 | async-start | bytes 2621440 | tf_op jit(solution)/shard_map/all_to_all | solution.py:146
  67.5 20.1 %collective-permute-start.2 = (bf16[128,2048]{1,0:T(8,128)(2,1)S(1)}, bf16[128,2048]{1,0:T(8,128)(2,1)S(1)}, u32[]{:S(2)}, u32[]{:S(2)}) collective-permute-start(bf16[128,2048]{1,0:T(8,128)(2,1)S(1)} %fusion.8), channel_id=1, source_target_pairs={{0,16},{8,24},{16,32},{24,40},{32,48},{40,56},{48,64},{56,72},{64,... | collective-permute-start | bytes 1572872 | tf_op jit(solution)/shard_map/ppermute | solution.py:20
  121.2 20.2 %all-to-all-start.3 = ((bf16[8,40,2048]{2,1,0:T(8,128)(2,1)}), bf16[8,40,2048]{2,1,0:T(8,128)(2,1)S(1)}, u32[]{:S(2)}, u32[]{:S(2)}) async-start(bf16[8,40,2048]{2,1,0:T(8,128)(2,1)} %bitcast.23), calls=%async_computation.3 | async-start | bytes 2621440 | tf_op jit(solution)/shard_map/all_to_all | solution.py:146

commit v3 on v1

--- a/solution.py
+++ b/solution.py
@@ -1,6 +1,10 @@
+import functools
+
 import jax
 import jax.numpy as jnp
 from jax import lax
+from jax.experimental import pallas as pl
+from jax.experimental.pallas import tpu as pltpu
 from jax.sharding import PartitionSpec as P
 
 TICKS = 2
@@ -18,14 +22,60 @@
     return lax.ppermute(value, axis, pairs)
 
 
-def expert_half(rows, up_part, down_part):
-    hidden = jax.nn.gelu(
-        jnp.einsum("gsd,dh->gsh", rows, up_part, preferred_element_type=jnp.float32),
-        approximate=True,
-    ).astype(jnp.bfloat16)
-    return jnp.einsum(
-        "gsh,hd->gsd", hidden, down_part, preferred_element_type=jnp.float32
-    ).astype(jnp.bfloat16)
+def expert_kernel(x_ref, own_up_hbm, own_down_hbm, far_up_hbm, far_down_hbm, out_ref,
+                  own_up, own_down, far_up, far_down, sems, *, block):
+    pairs = ((own_up_hbm, own_up), (far_up_hbm, far_up), (own_down_hbm, own_down), (far_down_hbm, far_down))
+    copies = [pltpu.make_async_copy(src, dst, sems.at[i]) for i, (src, dst) in enumerate(pairs)]
+    for copy in copies:
+        copy.start()
+    rows = x_ref[...]
+
+    def hidden_of(up_ref):
+        return jax.nn.gelu(
+            jnp.dot(rows, up_ref[...], preferred_element_type=jnp.float32), approximate=True
+        ).astype(jnp.bfloat16)
+
+    copies[0].wait()
+    own_hidden = hidden_of(own_up)
+    copies[1].wait()
+    far_hidden = hidden_of(far_up)
+    copies[2].wait()
+    copies[3].wait()
+    width = out_ref.shape[1]
+    for start in range(0, width, block):
+        cols = pl.ds(start, block)
+        own_part = jnp.dot(own_hidden, own_down[:, cols], preferred_element_type=jnp.float32)
+        far_part = jnp.dot(far_hidden, far_down[:, cols], preferred_element_type=jnp.float32)
+        total = own_part.astype(jnp.bfloat16).astype(jnp.float32) + far_part.astype(
+            jnp.bfloat16
+        ).astype(jnp.float32)
+        out_ref[:, cols] = total.astype(out_ref.dtype)
+
+
+def expert_full(rows, own_up, own_down, far_up, far_down, block=512):
+    count, width = rows.shape
+    hidden = own_up.shape[1]
+    cost = pl.CostEstimate(
+        flops=2 * 2 * count * width * hidden * 2,
+        transcendentals=count * hidden * 2,
+        bytes_accessed=4 * width * hidden * 2 + 2 * count * width * 2,
+    )
+    weight = pl.BlockSpec(memory_space=pl.ANY)
+    return pl.pallas_call(
+        functools.partial(expert_kernel, block=block),
+        in_specs=[pl.BlockSpec(memory_space=pltpu.VMEM), weight, weight, weight, weight],
+        out_specs=pl.BlockSpec(memory_space=pltpu.VMEM),
+        out_shape=jax.ShapeDtypeStruct((count, width), jnp.bfloat16),
+        scratch_shapes=[
+            pltpu.VMEM(own_up.shape, own_up.dtype),
+            pltpu.VMEM(own_down.shape, own_down.dtype),
+            pltpu.VMEM(far_up.shape, far_up.dtype),
+            pltpu.VMEM(far_down.shape, far_down.dtype),
+            pltpu.SemaphoreType.DMA((4,)),
+        ],
+        compiler_params=pltpu.CompilerParams(vmem_limit_bytes=48 * 1024 * 1024),
+        cost_estimate=cost,
+    )(rows, own_up, own_down, far_up, far_down)
 
 
 def slot_tables(ids, groups, slots):
@@ -49,6 +99,7 @@
     top = routes.shape[2]
     groups = lax.axis_size("expert")
     slots = min(rows, rows * top * 9 // (8 * groups))
+    slots = -(-slots // 8) * 8
     up_local = up_weight.reshape(up_weight.shape[2], up_weight.shape[3])
     down_local = down_weight.reshape(down_weight.shape[2], down_weight.shape[3])
     partner_up, partner_down = swapped((up_local, down_local), "section", 0)
@@ -68,10 +119,9 @@
             "gsr,rd->gsd", dispatch, normed, preferred_element_type=jnp.float32
         ).astype(jnp.bfloat16)
         received = lax.all_to_all(outgoing, "expert", split_axis=0, concat_axis=0, tiled=True)
-        own_part = lax.optimization_barrier(expert_half(received, up_local, down_local))
-        other_part = lax.optimization_barrier(expert_half(received, partner_up, partner_down))
-        summed = own_part.astype(jnp.float32) + other_part.astype(jnp.float32)
-        expert_out = summed.astype(jnp.bfloat16)
+        expert_out = expert_full(
+            received.reshape(groups * slots, -1), up_local, down_local, partner_up, partner_down
+        ).reshape(groups, slots, -1)
         answers = lax.all_to_all(expert_out, "expert", split_axis=0, concat_axis=0, tiled=True)
         total = state_f
         for k in range(top):

time: 145 us -> 134 us (0.924)
  matrix products: 22.6 us -> 5.34 us
  Pallas kernels: 0 us -> 11.3 us
  other arithmetic: 7.22 us -> 1.69 us
    dot_general x4 -> x0, matrix products: 18.2 us -> none  [expert_half(): jnp.einsum('gsh,hd->gsd', hidden, down_part, preferred_element_type=jnp.f...]
    pallas_call x0 -> x2, Pallas kernels: none -> 11.3 us  [expert_full(): pl.pallas_call(functools.partial(expert_kernel, block=block), in_specs=[p...]
    convert_element_type x2 -> x0, other arithmetic: 5.52 us -> none  [body(): expert_out = summed.astype(jnp.bfloat16)]
  transfers between devices with their start and end apart: 5 -> 5, of which waited for: 3 -> 3; matrix products, arithmetic and copies ran while one was open for 6% -> 3% of each run, Pallas kernels for 0% -> 0%
where the time goes in v3:
time: 134 us; the launch traced here: 133 us
  waiting for transfers between devices  49.7 us (37%)
  blocking collectives  48.3 us (36%)
  starting transfers between devices  15 us (11%)
  Pallas kernels  11.3 us (8%)
  matrix products  5.34 us (4%)
  other arithmetic  1.69 us (1%)
  local copies, waits for them, and re-layouts  1.61 us (1%)
    all_to_all x2, blocking collectives, body(): lax.all_to_all(outgoing, 'expert', split_axis=0, concat_axis=0, tiled=True)  48.3 us
    all_to_all x2, waiting for transfers between devices, body(): lax.all_to_all(expert_out, 'expert', split_axis=0, concat_axis=0, tiled=T...  31.6 us
    ppermute x1, waiting for transfers between devices, shifted(): return lax.ppermute(value, axis, pairs)  18.1 us
    pallas_call x2, Pallas kernels, expert_full(): pl.pallas_call(functools.partial(expert_kernel, block=block), in_specs=[p...  11.3 us
    all_to_all x2, starting transfers between devices, body(): lax.all_to_all(expert_out, 'expert', split_axis=0, concat_axis=0, tiled=T...  8.61 us
    ppermute x2, starting transfers between devices, swapped(): return lax.ppermute(value, axis, pairs)  4.45 us
    dot_general x4, matrix products, body(): jnp.einsum('gsr,gsd->rd', select[k], answers, preferred_element_type=jnp....  3.8 us
  transfers between devices with their start and end apart: 5, of which 3 were waited for; matrix products, arithmetic and copies ran while one was open for 3% of the time, Pallas kernels for 0%

profile of v3, /device:TPU:8, one launch (start us, length us, event | category | flops | bytes accessed | tf_op | source)
XLA Modules:
  0.0 133.2 jit_solution(5962358619185098195)
XLA Ops:
  0.0 2.0 %collective-permute-start = (bf16[2048,512]{1,0:T(8,128)(2,1)}, bf16[2048,512]{1,0:T(8,128)(2,1)}, u32[]{:S(2)}, u32[]{:S(2)}) collective-permute-start(bf16[2048,512]{1,0:T(8,128)(2,1)} %bitcast.80), channel_id=1, source_target_pairs={{0,8},{8,0},{16,24},{24,16},{32,40},{40,32},{48,56},{56,48},{64,72... | collective-permute-start | bytes 6291464 | tf_op jit(solution)/shard_map/ppermute | solution.py:16
  2.1 2.4 %collective-permute-start.1 = (bf16[512,2048]{1,0:T(8,128)(2,1)}, bf16[512,2048]{1,0:T(8,128)(2,1)}, u32[]{:S(2)}, u32[]{:S(2)}) collective-permute-start(bf16[512,2048]{1,0:T(8,128)(2,1)} %bitcast.85), channel_id=1, source_target_pairs={{0,8},{8,0},{16,24},{24,16},{32,40},{40,32},{48,56},{56,48},{64,72... | collective-permute-start | bytes 6291464 | tf_op jit(solution)/shard_map/ppermute | solution.py:16
  4.5 0.7 slice_bitcast_fusion.13
  5.2 0.1 copy.6
  5.3 0.1 eq.105
  5.4 0.2 fusion.10
  5.6 0.1 convert_element_type.66
  5.8 0.1 copy.7
  5.9 1.2 fusion.12
  7.2 0.6 convolution_convert_fusion.1
  7.8 0.0 copy-start
  7.8 26.2 %all_to_all.20 = bf16[8,40,2048]{2,1,0:T(8,128)(2,1)S(1)} all-to-all(bf16[8,40,2048]{2,1,0:T(8,128)(2,1)S(1)} %convolution_convert_fusion.1), channel_id=1, replica_groups=mesh['section'=64,'expert'=8] {'expert'}, dimensions={0} | all-to-all | bytes 2621440 | tf_op jit(solution)/shard_map/all_to_all | solution.py:121
  33.9 5.7 %shard_map.55 = bf16[320,2048]{1,0:T(8,128)(2,1)} custom-call(bf16[320,2048]{1,0:T(8,128)(2,1)S(1)} %bitcast.83, bf16[2048,512]{1,0:T(8,128)(2,1)S(1)} %bitcast.81, bf16[512,2048]{1,0:T(8,128)(2,1)} %bitcast.86, bf16[2048,512]{1,0:T(8,128)(2,1)} %collective-permute-done.far_up_hbm, bf16[512,2048]{1,0:T(8,128)(2,1)} %collective-permute-done.1.far_down_hbm), custom_call_target="tpu_custom_call" | custom-call | flops 2684354560 | bytes 11010048 | tf_op jit(solution)/shard_map/pallas_call | solution.py:64
  39.6 4.3 %all-to-all-start.1 = ((bf16[8,40,2048]{2,1,0:T(8,128)(2,1)}), bf16[8,40,2048]{2,1,0:T(8,128)(2,1)S(1)}, u32[]{:S(2)}, u32[]{:S(2)}) async-start(bf16[8,40,2048]{2,1,0:T(8,128)(2,1)} %bitcast.10), calls=%async_computation.1 | async-start | bytes 2621440 | tf_op jit(solution)/shard_map/all_to_all | solution.py:125
  43.9 0.1 copy.8
  44.0 0.1 eq.115
  44.2 0.2 fusion.11
  44.4 0.1 convert_element_type.75
  44.5 0.1 copy.9
  44.7 15.7 %all-to-all-done.1 = bf16[8,40,2048]{2,1,0:T(8,128)(2,1)S(1)} async-done(((bf16[8,40,2048]{2,1,0:T(8,128)(2,1)}), bf16[8,40,2048]{2,1,0:T(8,128)(2,1)S(1)}, u32[]{:S(2)}, u32[]{:S(2)}) %all-to-all-start.1) | async-done | bytes 1310752 | tf_op jit(solution)/shard_map/all_to_all | solution.py:125
  60.4 1.5 %fusion.7 = f32[128,2048]{1,0:T(8,128)S(1)} fusion(bf16[8,40,2048]{2,1,0:T(8,128)(2,1)S(1)} %all-to-all-done.1, bf16[128,2048]{1,0:T(8,128)(2,1)} %param.5, f32[128]{0:T(128)S(1)} %get-tuple-element.16, pred[2,8,40,128]{3,2,1,0:T(8,128)(4,1)S(1)} %broadcast_and_fusion.1), kind=kOutput, calls=%fused_computation.13 | convolution fusion | flops 168558592 | bytes 2925056 | tf_op jit(solution)/shard_map/gsr,gsd->rd/dot_general | solution.py:128
  61.9 0.5 fusion.8
  62.4 1.9 %collective-permute-start.2 = (bf16[128,2048]{1,0:T(8,128)(2,1)S(1)}, bf16[128,2048]{1,0:T(8,128)(2,1)S(1)}, u32[]{:S(2)}, u32[]{:S(2)}) collective-permute-start(bf16[128,2048]{1,0:T(8,128)(2,1)S(1)} %fusion.8), channel_id=1, source_target_pairs={{0,16},{8,24},{16,32},{24,40},{32,48},{40,56},{48,64},{56,72},{64,... | collective-permute-start | bytes 1572872 | tf_op jit(solution)/shard_map/ppermute | solution.py:22
  64.5 18.1 %collective-permute-done.2 = bf16[128,2048]{1,0:T(8,128)(2,1)S(1)} collective-permute-done((bf16[128,2048]{1,0:T(8,128)(2,1)S(1)}, bf16[128,2048]{1,0:T(8,128)(2,1)S(1)}, u32[]{:S(2)}, u32[]{:S(2)}) %collective-permute-start.2) | collective-permute-done | bytes 524320 | tf_op jit(solution)/shard_map/ppermute | solution.py:22
  82.5 0.2 fusion.14
  82.7 0.6 convolution_convert_fusion
  83.3 22.2 %all_to_all.21 = bf16[8,40,2048]{2,1,0:T(8,128)(2,1)S(1)} all-to-all(bf16[8,40,2048]{2,1,0:T(8,128)(2,1)S(1)} %convolution_convert_fusion), channel_id=1, replica_groups=mesh['section'=64,'expert'=8] {'expert'}, dimensions={0} | all-to-all | bytes 2621440 | tf_op jit(solution)/shard_map/all_to_all | solution.py:121
  105.5 5.7 %shard_map.56 = bf16[320,2048]{1,0:T(8,128)(2,1)} custom-call(bf16[320,2048]{1,0:T(8,128)(2,1)S(1)} %bitcast.84, bf16[2048,512]{1,0:T(8,128)(2,1)S(1)} %bitcast.82, bf16[512,2048]{1,0:T(8,128)(2,1)} %bitcast.87, bf16[2048,512]{1,0:T(8,128)(2,1)} %collective-permute-done.far_up_hbm, bf16[512,2048]{1,0:T(8,128)(2,1)} %collective-permute-done.1.far_down_hbm), custom_call_target="tpu_custom_call" | custom-call | flops 2684354560 | bytes 11010048 | tf_op jit(solution)/shard_map/pallas_call | solution.py:64
  111.1 4.3 %all-to-all-start.3 = ((bf16[8,40,2048]{2,1,0:T(8,128)(2,1)}), bf16[8,40,2048]{2,1,0:T(8,128)(2,1)S(1)}, u32[]{:S(2)}, u32[]{:S(2)}) async-start(bf16[8,40,2048]{2,1,0:T(8,128)(2,1)} %bitcast.23), calls=%async_computation.3 | async-start | bytes 2621440 | tf_op jit(solution)/shard_map/all_to_all | solution.py:125
  115.5 15.9 %all-to-all-done.3 = bf16[8,40,2048]{2,1,0:T(8,128)(2,1)S(1)} async-done(((bf16[8,40,2048]{2,1,0:T(8,128)(2,1)}), bf16[8,40,2048]{2,1,0:T(8,128)(2,1)S(1)}, u32[]{:S(2)}, u32[]{:S(2)}) %all-to-all-start.3) | async-done | bytes 1310752 | tf_op jit(solution)/shard_map/all_to_all | solution.py:125
  131.4 0.5 fusion
  131.9 1.3 fusion.9
  (23 shorter events, 0.3 us)
Async XLA Ops:
  0.0 7.2 %copy-start.1 = (bf16[128,2048]{1,0:T(8,128)(2,1)S(1)}, bf16[128,2048]{1,0:T(8,128)(2,1)}, u32[]{:S(2)}) copy-start(bf16[128,2048]{1,0:T(8,128)(2,1)} %param.5) | copy-start | bytes 1572868
  0.0 33.9 %collective-permute-start = (bf16[2048,512]{1,0:T(8,128)(2,1)}, bf16[2048,512]{1,0:T(8,128)(2,1)}, u32[]{:S(2)}, u32[]{:S(2)}) collective-permute-start(bf16[2048,512]{1,0:T(8,128)(2,1)} %bitcast.80), channel_id=1, source_target_pairs={{0,8},{8,0},{16,24},{24,16},{32,40},{40,32},{48,56},{56,48},{64,72... | collective-permute-start | bytes 6291464 | tf_op jit(solution)/shard_map/ppermute | solution.py:16
  2.1 31.9 %collective-permute-start.1 = (bf16[512,2048]{1,0:T(8,128)(2,1)}, bf16[512,2048]{1,0:T(8,128)(2,1)}, u32[]{:S(2)}, u32[]{:S(2)}) collective-permute-start(bf16[512,2048]{1,0:T(8,128)(2,1)} %bitcast.85), channel_id=1, source_target_pairs={{0,8},{8,0},{16,24},{24,16},{32,40},{40,32},{48,56},{56,48},{64,72... | collective-permute-start | bytes 6291464 | tf_op jit(solution)/shard_map/ppermute | solution.py:16
  7.8 26.2 %copy-start = (bf16[1,1,2048,512]{3,2,1,0:T(8,128)(2,1)S(1)}, bf16[1,1,2048,512]{3,2,1,0:T(8,128)(2,1)}, u32[]{:S(2)}) copy-start(bf16[1,1,2048,512]{3,2,1,0:T(8,128)(2,1)} %param.8) | copy-start | bytes 6291460
  39.6 5.0 %copy-start.2 = (f32[2,128,2]{1,2,0:T(2,128)S(1)}, f32[2,128,2]{1,2,0:T(2,128)}, u32[]{:S(2)}) copy-start(f32[2,128,2]{1,2,0:T(2,128)} %param.7) | copy-start | bytes 6148
  39.6 20.8 %all-to-all-start.1 = ((bf16[8,40,2048]{2,1,0:T(8,128)(2,1)}), bf16[8,40,2048]{2,1,0:T(8,128)(2,1)S(1)}, u32[]{:S(2)}, u32[]{:S(2)}) async-start(bf16[8,40,2048]{2,1,0:T(8,128)(2,1)} %bitcast.10), calls=%async_computation.1 | async-start | bytes 2621440 | tf_op jit(solution)/shard_map/all_to_all | solution.py:125
  62.4 20.1 %collective-permute-start.2 = (bf16[128,2048]{1,0:T(8,128)(2,1)S(1)}, bf16[128,2048]{1,0:T(8,128)(2,1)S(1)}, u32[]{:S(2)}, u32[]{:S(2)}) collective-permute-start(bf16[128,2048]{1,0:T(8,128)(2,1)S(1)} %fusion.8), channel_id=1, source_target_pairs={{0,16},{8,24},{16,32},{24,40},{32,48},{40,56},{48,64},{56,72},{64,... | collective-permute-start | bytes 1572872 | tf_op jit(solution)/shard_map/ppermute | solution.py:22
  111.1 20.2 %all-to-all-start.3 = ((bf16[8,40,2048]{2,1,0:T(8,128)(2,1)}), bf16[8,40,2048]{2,1,0:T(8,128)(2,1)S(1)}, u32[]{:S(2)}, u32[]{:S(2)}) async-start(bf16[8,40,2048]{2,1,0:T(8,128)(2,1)} %bitcast.23), calls=%async_computation.3 | async-start | bytes 2621440 | tf_op jit(solution)/shard_map/all_to_all | solution.py:125

commit v4 on v3

--- a/solution.py
+++ b/solution.py
@@ -78,6 +78,57 @@
     )(rows, own_up, own_down, far_up, far_down)
 
 
+def dispatch_kernel(state_ref, select_ref, out_ref):
+    state = state_ref[...].astype(jnp.float32)
+    scale = lax.rsqrt(jnp.mean(state * state, axis=1, keepdims=True) + 1e-06)
+    normed = (state * scale).astype(jnp.bfloat16)
+    out_ref[...] = jnp.dot(select_ref[...], normed, preferred_element_type=jnp.float32).astype(
+        out_ref.dtype
+    )
+
+
+def dispatch_rows(state, select):
+    count = select.shape[0]
+    width = state.shape[1]
+    vmem = pl.BlockSpec(memory_space=pltpu.VMEM)
+    return pl.pallas_call(
+        dispatch_kernel,
+        in_specs=[vmem, vmem],
+        out_specs=vmem,
+        out_shape=jax.ShapeDtypeStruct((count, width), jnp.bfloat16),
+        cost_estimate=pl.CostEstimate(
+            flops=2 * count * state.shape[0] * width,
+            transcendentals=state.shape[0],
+            bytes_accessed=2 * (count + state.shape[0]) * width,
+        ),
+    )(state, select)
+
+
+def combine_kernel(state_ref, answers_ref, pick_ref, share_ref, out_ref):
+    total = state_ref[...].astype(jnp.float32)
+    answers = answers_ref[...]
+    for k in range(pick_ref.shape[0]):
+        picked = jnp.dot(pick_ref[k], answers, preferred_element_type=jnp.float32)
+        total = total + share_ref[:, k : k + 1] * picked
+    out_ref[...] = total.astype(out_ref.dtype)
+
+
+def combine_rows(state, answers, pick, share):
+    rows, width = state.shape
+    vmem = pl.BlockSpec(memory_space=pltpu.VMEM)
+    return pl.pallas_call(
+        combine_kernel,
+        in_specs=[vmem, vmem, vmem, vmem],
+        out_specs=vmem,
+        out_shape=jax.ShapeDtypeStruct((rows, width), state.dtype),
+        cost_estimate=pl.CostEstimate(
+            flops=2 * pick.shape[0] * rows * answers.shape[0] * width,
+            transcendentals=0,
+            bytes_accessed=2 * (2 * rows + answers.shape[0]) * width,
+        ),
+    )(state, answers, pick, share)
+
+
 def slot_tables(ids, groups, slots):
     rows, top = ids.shape
     flat = ids.reshape(-1)
@@ -109,27 +160,16 @@
             state = shifted(state, "section", 2)
         weights = combine[tick]
         select = slot_tables(routes[tick], groups, slots)
-        state_f = state.astype(jnp.float32)
-        normed = (
-            state_f * lax.rsqrt(jnp.mean(state_f * state_f, axis=1, keepdims=True) + 1e-06)
-        ).astype(jnp.bfloat16)
         share = weights / jnp.sum(weights, axis=1, keepdims=True)
-        dispatch = jnp.sum(select, axis=0)
-        outgoing = jnp.einsum(
-            "gsr,rd->gsd", dispatch, normed, preferred_element_type=jnp.float32
-        ).astype(jnp.bfloat16)
+        dispatch = jnp.sum(select, axis=0).reshape(groups * slots, rows)
+        outgoing = dispatch_rows(state, dispatch).reshape(groups, slots, -1)
         received = lax.all_to_all(outgoing, "expert", split_axis=0, concat_axis=0, tiled=True)
         expert_out = expert_full(
             received.reshape(groups * slots, -1), up_local, down_local, partner_up, partner_down
         ).reshape(groups, slots, -1)
         answers = lax.all_to_all(expert_out, "expert", split_axis=0, concat_axis=0, tiled=True)
-        total = state_f
-        for k in range(top):
-            picked = jnp.einsum(
-                "gsr,gsd->rd", select[k], answers, preferred_element_type=jnp.float32
-            )
-            total = total + share[:, k : k + 1] * picked
-        state = total.astype(jnp.bfloat16)
+        pick = jnp.swapaxes(select.reshape(top, groups * slots, rows), 1, 2)
+        state = combine_rows(state, answers.reshape(groups * slots, -1), pick, share)
     return state
 
 

time: 134 us -> 143 us (1.067)
  Pallas kernels: 11.3 us -> 22.9 us
  waiting for transfers between devices: 49.7 us -> 43.3 us
  local copies, waits for them, and re-layouts: 1.61 us -> 7.34 us
  matrix products: 5.34 us -> 0.4 us
  other arithmetic: 1.69 us -> 3.61 us
    pallas_call x0 -> x4, Pallas kernels: none -> 11.5 us  [the longest x2 6.02 us: combine_rows(): pl.pallas_call(combine_kernel, in_specs=[vmem, vmem, vmem, vmem], out_spe...]
    dot_general x6 -> x0, matrix products: 4.95 us -> none  [the longest x4 3.8 us: body(): jnp.einsum('gsr,gsd->rd', select[k], answers, preferred_element_type=jnp....]
    all_to_all x2, waiting for transfers between devices: 31.6 us -> 27.2 us  [body(): lax.all_to_all(expert_out, 'expert', split_axis=0, concat_axis=0, tiled=T...]
    unnamed x6 -> x12, local copies, waits for them, and re-layouts: 0.02 us -> 3.18 us
    transpose x0 -> x2, local copies, waits for them, and re-layouts: none -> 2.57 us  [body(): pick = jnp.swapaxes(select.reshape(top, groups * slots, rows), 1, 2)]
    ppermute x1, waiting for transfers between devices: 18.1 us -> 16.1 us  [shifted(): return lax.ppermute(value, axis, pairs)]
  transfers between devices with their start and end apart: 5 -> 5, of which waited for: 3 -> 3; matrix products, arithmetic and copies ran while one was open for 3% -> 6% of each run, Pallas kernels for 0% -> 2%
where the time goes in v4:
time: 143 us; the launch traced here: 142 us
  blocking collectives  49.7 us (35%)
  waiting for transfers between devices  43.3 us (30%)
  Pallas kernels  22.9 us (16%)
  starting transfers between devices  14.7 us (10%)
  local copies, waits for them, and re-layouts  7.34 us (5%)
  other arithmetic  3.61 us (3%)
    all_to_all x2, blocking collectives, body(): lax.all_to_all(outgoing, 'expert', split_axis=0, concat_axis=0, tiled=True)  49.7 us
    all_to_all x2, waiting for transfers between devices, body(): lax.all_to_all(expert_out, 'expert', split_axis=0, concat_axis=0, tiled=T...  27.2 us
    ppermute x1, waiting for transfers between devices, shifted(): return lax.ppermute(value, axis, pairs)  16.1 us
    pallas_call x2, Pallas kernels, expert_full(): pl.pallas_call(functools.partial(expert_kernel, block=block), in_specs=[p...  11.3 us
    all_to_all x2, starting transfers between devices, body(): lax.all_to_all(expert_out, 'expert', split_axis=0, concat_axis=0, tiled=T...  8.47 us
    pallas_call x2, Pallas kernels, combine_rows(): pl.pallas_call(combine_kernel, in_specs=[vmem, vmem, vmem, vmem], out_spe...  6.02 us
    pallas_call x2, Pallas kernels, dispatch_rows(): pl.pallas_call(dispatch_kernel, in_specs=[vmem, vmem], out_specs=vmem, ou...  5.53 us
    ppermute x2, starting transfers between devices, swapped(): return lax.ppermute(value, axis, pairs)  4.32 us
  transfers between devices with their start and end apart: 5, of which 3 were waited for; matrix products, arithmetic and copies ran while one was open for 6% of the time, Pallas kernels for 2%

profile of v4, /device:TPU:8, one launch (start us, length us, event | category | flops | bytes accessed | tf_op | source)
XLA Modules:
  0.0 142.0 jit_solution(5346526864348253144)
XLA Ops:
  0.0 1.9 %collective-permute-start = (bf16[2048,512]{1,0:T(8,128)(2,1)}, bf16[2048,512]{1,0:T(8,128)(2,1)}, u32[]{:S(2)}, u32[]{:S(2)}) collective-permute-start(bf16[2048,512]{1,0:T(8,128)(2,1)} %bitcast.30), channel_id=1, source_target_pairs={{0,8},{8,0},{16,24},{24,16},{32,40},{40,32},{48,56},{56,48},{64,72... | collective-permute-start | bytes 6291464 | tf_op jit(solution)/shard_map/ppermute | solution.py:16
  1.9 2.4 %collective-permute-start.1 = (bf16[512,2048]{1,0:T(8,128)(2,1)}, bf16[512,2048]{1,0:T(8,128)(2,1)}, u32[]{:S(2)}, u32[]{:S(2)}) collective-permute-start(bf16[512,2048]{1,0:T(8,128)(2,1)} %bitcast.35), channel_id=1, source_target_pairs={{0,8},{8,0},{16,24},{24,16},{32,40},{40,32},{48,56},{56,48},{64,72... | collective-permute-start | bytes 6291464 | tf_op jit(solution)/shard_map/ppermute | solution.py:16
  4.3 0.7 slice_bitcast_fusion
  5.2 0.1 eq.105
  5.3 0.2 fusion
  5.8 0.7 fusion.2
  6.4 2.8 %shard_map.55 = bf16[320,2048]{1,0:T(8,128)(2,1)} custom-call(bf16[128,2048]{1,0:T(8,128)(2,1)} %state_ref.3, bf16[320,128]{1,0:T(8,128)(2,1)} %bitcast.47), custom_call_target="tpu_custom_call" | custom-call | flops 167772160 | bytes 1835008 | tf_op jit(solution)/shard_map/pallas_call | solution.py:94
  9.2 27.2 %all_to_all.20 = bf16[8,40,2048]{2,1,0:T(8,128)(2,1)S(1)} all-to-all(bf16[8,40,2048]{2,1,0:T(8,128)(2,1)} %bitcast.40), channel_id=1, replica_groups=mesh['section'=64,'expert'=8] {'expert'}, dimensions={0} | all-to-all | bytes 2621440 | tf_op jit(solution)/shard_map/all_to_all | solution.py:166
  36.4 5.7 %shard_map.56 = bf16[320,2048]{1,0:T(8,128)(2,1)} custom-call(bf16[320,2048]{1,0:T(8,128)(2,1)S(1)} %bitcast.33, bf16[2048,512]{1,0:T(8,128)(2,1)S(1)} %bitcast.31, bf16[512,2048]{1,0:T(8,128)(2,1)} %bitcast.36, bf16[2048,512]{1,0:T(8,128)(2,1)} %collective-permute-done.far_up_hbm, bf16[512,2048]{1,0:T(8,128)(2,1)} %collective-permute-done.1.far_down_hbm), custom_call_target="tpu_custom_call" | custom-call | flops 2684354560 | bytes 11010048 | tf_op jit(solution)/shard_map/pallas_call | solution.py:64
  42.1 4.3 %all-to-all-start.1 = ((bf16[8,40,2048]{2,1,0:T(8,128)(2,1)}), bf16[8,40,2048]{2,1,0:T(8,128)(2,1)S(1)}, u32[]{:S(2)}, u32[]{:S(2)}) async-start(bf16[8,40,2048]{2,1,0:T(8,128)(2,1)} %bitcast.8), calls=%async_computation.1 | async-start | bytes 2621440 | tf_op jit(solution)/shard_map/all_to_all | solution.py:170
  46.4 0.7 and_convert_fusion.1
  47.1 1.7 %copy.10 = bf16[2,320,128]{1,2,0:T(8,128)(2,1)} copy(bf16[2,320,128]{2,1,0:T(8,128)(2,1)} %bitcast.44) | data formatting | bytes 327680 | tf_op jit(solution)/shard_map/transpose | solution.py:171
  49.0 0.7 bitcast_divide_fusion.1.share_ref
  49.7 13.2 %all-to-all-done.1 = bf16[8,40,2048]{2,1,0:T(8,128)(2,1)S(1)} async-done(((bf16[8,40,2048]{2,1,0:T(8,128)(2,1)}), bf16[8,40,2048]{2,1,0:T(8,128)(2,1)S(1)}, u32[]{:S(2)}, u32[]{:S(2)}) %all-to-all-start.1) | async-done | bytes 1310752 | tf_op jit(solution)/shard_map/all_to_all | solution.py:170
  62.9 1.1 copy-done.1
  63.9 3.0 %shard_map.57 = bf16[128,2048]{1,0:T(8,128)(2,1)} custom-call(bf16[128,2048]{1,0:T(8,128)(2,1)} %state_ref.3, bf16[320,2048]{1,0:T(8,128)(2,1)} %bitcast.38, bf16[2,128,320]{2,1,0:T(8,128)(2,1)} %bitcast.42, f32[128,2]{1,0:T(8,128)} %bitcast_divide_fusion.1.share_ref), custom_call_target="tpu_custom_call" | custom-call | flops 335544320 | bytes 2359296 | tf_op jit(solution)/shard_map/pallas_call | solution.py:119
  67.0 1.9 %collective-permute-start.2 = (bf16[128,2048]{1,0:T(8,128)(2,1)}, bf16[128,2048]{1,0:T(8,128)(2,1)S(1)}, u32[]{:S(2)}, u32[]{:S(2)}) collective-permute-start(bf16[128,2048]{1,0:T(8,128)(2,1)} %shard_map.57), channel_id=1, source_target_pairs={{0,16},{8,24},{16,32},{24,40},{32,48},{40,56},{48,64},{56,72},{64,... | collective-permute-start | bytes 1572872 | tf_op jit(solution)/shard_map/ppermute | solution.py:22
  69.0 0.1 eq.115
  69.1 0.2 fusion.1
  69.3 0.1 convert_element_type.55
  69.6 0.7 fusion.3
  70.3 16.1 %collective-permute-done.2.state_ref = bf16[128,2048]{1,0:T(8,128)(2,1)S(1)} collective-permute-done((bf16[128,2048]{1,0:T(8,128)(2,1)}, bf16[128,2048]{1,0:T(8,128)(2,1)S(1)}, u32[]{:S(2)}, u32[]{:S(2)}) %collective-permute-start.2) | collective-permute-done | bytes 524320 | tf_op jit(solution)/shard_map/ppermute | solution.py:22
  86.4 0.8 copy-done.3
  87.2 2.8 %shard_map.58 = bf16[320,2048]{1,0:T(8,128)(2,1)} custom-call(bf16[128,2048]{1,0:T(8,128)(2,1)} %copy-done.3, bf16[320,128]{1,0:T(8,128)(2,1)} %bitcast.46), custom_call_target="tpu_custom_call" | custom-call | flops 167772160 | bytes 1835008 | tf_op jit(solution)/shard_map/pallas_call | solution.py:94
  90.0 22.5 %all_to_all.21 = bf16[8,40,2048]{2,1,0:T(8,128)(2,1)S(1)} all-to-all(bf16[8,40,2048]{2,1,0:T(8,128)(2,1)} %bitcast.41), channel_id=1, replica_groups=mesh['section'=64,'expert'=8] {'expert'}, dimensions={0} | all-to-all | bytes 2621440 | tf_op jit(solution)/shard_map/all_to_all | solution.py:166
  112.5 5.7 %shard_map.59 = bf16[320,2048]{1,0:T(8,128)(2,1)} custom-call(bf16[320,2048]{1,0:T(8,128)(2,1)S(1)} %bitcast.34, bf16[2048,512]{1,0:T(8,128)(2,1)S(1)} %bitcast.32, bf16[512,2048]{1,0:T(8,128)(2,1)} %bitcast.37, bf16[2048,512]{1,0:T(8,128)(2,1)} %collective-permute-done.far_up_hbm, bf16[512,2048]{1,0:T(8,128)(2,1)} %collective-permute-done.1.far_down_hbm), custom_call_target="tpu_custom_call" | custom-call | flops 2684354560 | bytes 11010048 | tf_op jit(solution)/shard_map/pallas_call | solution.py:64
  118.1 4.2 %all-to-all-start.3 = ((bf16[8,40,2048]{2,1,0:T(8,128)(2,1)}), bf16[8,40,2048]{2,1,0:T(8,128)(2,1)S(1)}, u32[]{:S(2)}, u32[]{:S(2)}) async-start(bf16[8,40,2048]{2,1,0:T(8,128)(2,1)} %bitcast.19), calls=%async_computation.3 | async-start | bytes 2621440 | tf_op jit(solution)/shard_map/all_to_all | solution.py:170
  122.4 0.8 copy.14
  123.3 0.7 bitcast_divide_fusion.share_ref
  124.0 14.0 %all-to-all-done.3 = bf16[8,40,2048]{2,1,0:T(8,128)(2,1)S(1)} async-done(((bf16[8,40,2048]{2,1,0:T(8,128)(2,1)}), bf16[8,40,2048]{2,1,0:T(8,128)(2,1)S(1)}, u32[]{:S(2)}, u32[]{:S(2)}) %all-to-all-start.3) | async-done | bytes 1310752 | tf_op jit(solution)/shard_map/all_to_all | solution.py:170
  138.0 1.1 copy-done.2
  139.0 3.0 %shard_map.60 = bf16[128,2048]{1,0:T(8,128)(2,1)} custom-call(bf16[128,2048]{1,0:T(8,128)(2,1)} %copy-done.3, bf16[320,2048]{1,0:T(8,128)(2,1)} %bitcast.39, bf16[2,128,320]{2,1,0:T(8,128)(2,1)} %bitcast.43, f32[128,2]{1,0:T(8,128)} %bitcast_divide_fusion.share_ref), custom_call_target="tpu_custom_call" | custom-call | flops 335544320 | bytes 2359296 | tf_op jit(solution)/shard_map/pallas_call | solution.py:119
  (23 shorter events, 0.9 us)
Async XLA Ops:
  0.0 36.4 %collective-permute-start = (bf16[2048,512]{1,0:T(8,128)(2,1)}, bf16[2048,512]{1,0:T(8,128)(2,1)}, u32[]{:S(2)}, u32[]{:S(2)}) collective-permute-start(bf16[2048,512]{1,0:T(8,128)(2,1)} %bitcast.30), channel_id=1, source_target_pairs={{0,8},{8,0},{16,24},{24,16},{32,40},{40,32},{48,56},{56,48},{64,72... | collective-permute-start | bytes 6291464 | tf_op jit(solution)/shard_map/ppermute | solution.py:16
  1.9 34.5 %collective-permute-start.1 = (bf16[512,2048]{1,0:T(8,128)(2,1)}, bf16[512,2048]{1,0:T(8,128)(2,1)}, u32[]{:S(2)}, u32[]{:S(2)}) collective-permute-start(bf16[512,2048]{1,0:T(8,128)(2,1)} %bitcast.35), channel_id=1, source_target_pairs={{0,8},{8,0},{16,24},{24,16},{32,40},{40,32},{48,56},{56,48},{64,72... | collective-permute-start | bytes 6291464 | tf_op jit(solution)/shard_map/ppermute | solution.py:16
  9.2 27.2 %copy-start = (bf16[1,1,2048,512]{3,2,1,0:T(8,128)(2,1)S(1)}, bf16[1,1,2048,512]{3,2,1,0:T(8,128)(2,1)}, u32[]{:S(2)}) copy-start(bf16[1,1,2048,512]{3,2,1,0:T(8,128)(2,1)} %param.8) | copy-start | bytes 6291460
  42.1 6.8 %copy-start.4 = (f32[2,128,2]{1,2,0:T(2,128)S(1)}, f32[2,128,2]{1,2,0:T(2,128)}, u32[]{:S(2)}) copy-start(f32[2,128,2]{1,2,0:T(2,128)} %param.7) | copy-start | bytes 6148
  42.1 20.8 %all-to-all-start.1 = ((bf16[8,40,2048]{2,1,0:T(8,128)(2,1)}), bf16[8,40,2048]{2,1,0:T(8,128)(2,1)S(1)}, u32[]{:S(2)}, u32[]{:S(2)}) async-start(bf16[8,40,2048]{2,1,0:T(8,128)(2,1)} %bitcast.8), calls=%async_computation.1 | async-start | bytes 2621440 | tf_op jit(solution)/shard_map/all_to_all | solution.py:170
  62.9 1.1 copy-start.1
  67.0 19.4 %collective-permute-start.2 = (bf16[128,2048]{1,0:T(8,128)(2,1)}, bf16[128,2048]{1,0:T(8,128)(2,1)S(1)}, u32[]{:S(2)}, u32[]{:S(2)}) collective-permute-start(bf16[128,2048]{1,0:T(8,128)(2,1)} %shard_map.57), channel_id=1, source_target_pairs={{0,16},{8,24},{16,32},{24,40},{32,48},{40,56},{48,64},{56,72},{64,... | collective-permute-start | bytes 1572872 | tf_op jit(solution)/shard_map/ppermute | solution.py:22
  86.4 0.8 copy-start.3
  118.1 19.8 %all-to-all-start.3 = ((bf16[8,40,2048]{2,1,0:T(8,128)(2,1)}), bf16[8,40,2048]{2,1,0:T(8,128)(2,1)S(1)}, u32[]{:S(2)}, u32[]{:S(2)}) async-start(bf16[8,40,2048]{2,1,0:T(8,128)(2,1)} %bitcast.19), calls=%async_computation.3 | async-start | bytes 2621440 | tf_op jit(solution)/shard_map/all_to_all | solution.py:170
  138.0 1.1 copy-start.2

commit v5 on v3

--- a/solution.py
+++ b/solution.py
@@ -110,9 +110,10 @@
         weights = combine[tick]
         select = slot_tables(routes[tick], groups, slots)
         state_f = state.astype(jnp.float32)
-        normed = (
-            state_f * lax.rsqrt(jnp.mean(state_f * state_f, axis=1, keepdims=True) + 1e-06)
-        ).astype(jnp.bfloat16)
+        gram = jnp.dot(state, state.T, preferred_element_type=jnp.float32)
+        eye = jnp.arange(rows)[:, None] == jnp.arange(rows)[None, :]
+        squares = jnp.sum(jnp.where(eye, gram, 0.0), axis=1, keepdims=True)
+        normed = (state_f * lax.rsqrt(squares / state.shape[1] + 1e-06)).astype(jnp.bfloat16)
         share = weights / jnp.sum(weights, axis=1, keepdims=True)
         dispatch = jnp.sum(select, axis=0)
         outgoing = jnp.einsum(

time: 134 us -> 134 us (level)
  matrix products: 5.34 us -> 7.18 us
  other arithmetic: 1.69 us -> 0.28 us
    dot_general x0 -> x2, matrix products: none -> 1.83 us  [body(): gram = jnp.dot(state, state.T, preferred_element_type=jnp.float32)]
    reduce_sum x2 -> x0, other arithmetic: 1.42 us -> none  [body(): jnp.mean(state_f * state_f, axis=1, keepdims=True) + 1e-06]
where the time goes in v5:
time: 134 us
  waiting for transfers between devices  49.7 us (37%)
  blocking collectives  48.3 us (36%)
  starting transfers between devices  15 us (11%)
  Pallas kernels  11.3 us (8%)
  matrix products  7.18 us (5%)
  local copies, waits for them, and re-layouts  1.61 us (1%)
    all_to_all x2, blocking collectives, body(): lax.all_to_all(outgoing, 'expert', split_axis=0, concat_axis=0, tiled=True)  48.3 us
    all_to_all x2, waiting for transfers between devices, body(): lax.all_to_all(expert_out, 'expert', split_axis=0, concat_axis=0, tiled=T...  31.6 us
    ppermute x1, waiting for transfers between devices, shifted(): return lax.ppermute(value, axis, pairs)  18.1 us
    pallas_call x2, Pallas kernels, expert_full(): pl.pallas_call(functools.partial(expert_kernel, block=block), in_specs=[p...  11.3 us
    all_to_all x2, starting transfers between devices, body(): lax.all_to_all(expert_out, 'expert', split_axis=0, concat_axis=0, tiled=T...  8.61 us
    ppermute x2, starting transfers between devices, swapped(): return lax.ppermute(value, axis, pairs)  4.45 us
    dot_general x4, matrix products, body(): jnp.einsum('gsr,gsd->rd', select[k], answers, preferred_element_type=jnp....  3.81 us
  transfers between devices with their start and end apart: 5, of which 3 were waited for; matrix products, arithmetic and copies ran while one was open for 3% of the time, Pallas kernels for 0%

profile of v5, /device:TPU:8, one launch (start us, length us, event | category | flops | bytes accessed | tf_op | source)
XLA Modules:
  0.0 133.6 jit_solution(13955518922491200886)
XLA Ops:
  0.0 2.0 %collective-permute-start = (bf16[2048,512]{1,0:T(8,128)(2,1)}, bf16[2048,512]{1,0:T(8,128)(2,1)}, u32[]{:S(2)}, u32[]{:S(2)}) collective-permute-start(bf16[2048,512]{1,0:T(8,128)(2,1)} %bitcast.84), channel_id=1, source_target_pairs={{0,8},{8,0},{16,24},{24,16},{32,40},{40,32},{48,56},{56,48},{64,72... | collective-permute-start | bytes 6291464 | tf_op jit(solution)/shard_map/ppermute | solution.py:16
  2.1 2.4 %collective-permute-start.1 = (bf16[512,2048]{1,0:T(8,128)(2,1)}, bf16[512,2048]{1,0:T(8,128)(2,1)}, u32[]{:S(2)}, u32[]{:S(2)}) collective-permute-start(bf16[512,2048]{1,0:T(8,128)(2,1)} %bitcast.89), channel_id=1, source_target_pairs={{0,8},{8,0},{16,24},{24,16},{32,40},{40,32},{48,56},{56,48},{64,72... | collective-permute-start | bytes 6291464 | tf_op jit(solution)/shard_map/ppermute | solution.py:16
  4.5 0.7 slice_bitcast_fusion.13
  5.2 0.1 copy.10
  5.3 0.1 eq.131
  5.4 0.2 fusion.12
  5.6 0.1 convert_element_type.66
  5.8 0.1 copy.11
  5.9 1.5 %fusion.10 = f32[128]{0:T(128)S(1)} fusion(bf16[128,2048]{1,0:T(8,128)(2,1)} %param.5), kind=kOutput, calls=%fused_computation.20 | convolution fusion | flops 67157888 | bytes 524800 | tf_op jit(solution)/shard_map/dot_general | solution.py:113
  7.5 0.6 convolution_convert_fusion.1
  8.1 0.0 copy-start
  8.1 26.1 %all_to_all.20 = bf16[8,40,2048]{2,1,0:T(8,128)(2,1)S(1)} all-to-all(bf16[8,40,2048]{2,1,0:T(8,128)(2,1)S(1)} %convolution_convert_fusion.1), channel_id=1, replica_groups=mesh['section'=64,'expert'=8] {'expert'}, dimensions={0} | all-to-all | bytes 2621440 | tf_op jit(solution)/shard_map/all_to_all | solution.py:122
  34.2 5.7 %shard_map.55 = bf16[320,2048]{1,0:T(8,128)(2,1)} custom-call(bf16[320,2048]{1,0:T(8,128)(2,1)S(1)} %bitcast.87, bf16[2048,512]{1,0:T(8,128)(2,1)S(1)} %bitcast.85, bf16[512,2048]{1,0:T(8,128)(2,1)} %bitcast.90, bf16[2048,512]{1,0:T(8,128)(2,1)} %collective-permute-done.far_up_hbm, bf16[512,2048]{1,0:T(8,128)(2,1)} %collective-permute-done.1.far_down_hbm), custom_call_target="tpu_custom_call" | custom-call | flops 2684354560 | bytes 11010048 | tf_op jit(solution)/shard_map/pallas_call | solution.py:64
  39.9 4.3 %all-to-all-start.1 = ((bf16[8,40,2048]{2,1,0:T(8,128)(2,1)}), bf16[8,40,2048]{2,1,0:T(8,128)(2,1)S(1)}, u32[]{:S(2)}, u32[]{:S(2)}) async-start(bf16[8,40,2048]{2,1,0:T(8,128)(2,1)} %bitcast.10), calls=%async_computation.1 | async-start | bytes 2621440 | tf_op jit(solution)/shard_map/all_to_all | solution.py:126
  44.2 0.1 copy.13
  44.3 0.1 eq.144
  44.5 0.2 fusion.13
  44.7 0.1 convert_element_type.75
  44.8 0.1 copy.14
  45.0 15.7 %all-to-all-done.1 = bf16[8,40,2048]{2,1,0:T(8,128)(2,1)S(1)} async-done(((bf16[8,40,2048]{2,1,0:T(8,128)(2,1)}), bf16[8,40,2048]{2,1,0:T(8,128)(2,1)S(1)}, u32[]{:S(2)}, u32[]{:S(2)}) %all-to-all-start.1) | async-done | bytes 1310752 | tf_op jit(solution)/shard_map/all_to_all | solution.py:126
  60.7 1.5 %fusion.7 = f32[128,2048]{1,0:T(8,128)S(1)} fusion(bf16[8,40,2048]{2,1,0:T(8,128)(2,1)S(1)} %all-to-all-done.1, bf16[128,2048]{1,0:T(8,128)(2,1)} %param.5, f32[128]{0:T(128)S(1)} %get-tuple-element.16, pred[2,8,40,128]{3,2,1,0:T(8,128)(4,1)S(1)} %broadcast_and_fusion.1), kind=kOutput, calls=%fused_computation.13 | convolution fusion | flops 168558592 | bytes 2925056 | tf_op jit(solution)/shard_map/gsr,gsd->rd/dot_general | solution.py:129
  62.2 0.5 fusion.8
  62.7 1.9 %collective-permute-start.2 = (bf16[128,2048]{1,0:T(8,128)(2,1)S(1)}, bf16[128,2048]{1,0:T(8,128)(2,1)S(1)}, u32[]{:S(2)}, u32[]{:S(2)}) collective-permute-start(bf16[128,2048]{1,0:T(8,128)(2,1)S(1)} %fusion.8), channel_id=1, source_target_pairs={{0,16},{8,24},{16,32},{24,40},{32,48},{40,56},{48,64},{56,72},{64,... | collective-permute-start | bytes 1572872 | tf_op jit(solution)/shard_map/ppermute | solution.py:22
  64.7 18.1 %collective-permute-done.2 = bf16[128,2048]{1,0:T(8,128)(2,1)S(1)} collective-permute-done((bf16[128,2048]{1,0:T(8,128)(2,1)S(1)}, bf16[128,2048]{1,0:T(8,128)(2,1)S(1)}, u32[]{:S(2)}, u32[]{:S(2)}) %collective-permute-start.2) | collective-permute-done | bytes 524320 | tf_op jit(solution)/shard_map/ppermute | solution.py:22
  82.8 0.3 fusion.11
  83.1 0.6 convolution_convert_fusion
  83.7 22.2 %all_to_all.21 = bf16[8,40,2048]{2,1,0:T(8,128)(2,1)S(1)} all-to-all(bf16[8,40,2048]{2,1,0:T(8,128)(2,1)S(1)} %convolution_convert_fusion), channel_id=1, replica_groups=mesh['section'=64,'expert'=8] {'expert'}, dimensions={0} | all-to-all | bytes 2621440 | tf_op jit(solution)/shard_map/all_to_all | solution.py:122
  105.9 5.7 %shard_map.56 = bf16[320,2048]{1,0:T(8,128)(2,1)} custom-call(bf16[320,2048]{1,0:T(8,128)(2,1)S(1)} %bitcast.88, bf16[2048,512]{1,0:T(8,128)(2,1)S(1)} %bitcast.86, bf16[512,2048]{1,0:T(8,128)(2,1)} %bitcast.91, bf16[2048,512]{1,0:T(8,128)(2,1)} %collective-permute-done.far_up_hbm, bf16[512,2048]{1,0:T(8,128)(2,1)} %collective-permute-done.1.far_down_hbm), custom_call_target="tpu_custom_call" | custom-call | flops 2684354560 | bytes 11010048 | tf_op jit(solution)/shard_map/pallas_call | solution.py:64
  111.6 4.3 %all-to-all-start.3 = ((bf16[8,40,2048]{2,1,0:T(8,128)(2,1)}), bf16[8,40,2048]{2,1,0:T(8,128)(2,1)S(1)}, u32[]{:S(2)}, u32[]{:S(2)}) async-start(bf16[8,40,2048]{2,1,0:T(8,128)(2,1)} %bitcast.23), calls=%async_computation.3 | async-start | bytes 2621440 | tf_op jit(solution)/shard_map/all_to_all | solution.py:126
  115.9 15.9 %all-to-all-done.3 = bf16[8,40,2048]{2,1,0:T(8,128)(2,1)S(1)} async-done(((bf16[8,40,2048]{2,1,0:T(8,128)(2,1)}), bf16[8,40,2048]{2,1,0:T(8,128)(2,1)S(1)}, u32[]{:S(2)}, u32[]{:S(2)}) %all-to-all-start.3) | async-done | bytes 1310752 | tf_op jit(solution)/shard_map/all_to_all | solution.py:126
  131.8 0.5 fusion
  132.3 1.3 fusion.9
  (23 shorter events, 0.3 us)
Async XLA Ops:
  0.0 7.5 %copy-start.1 = (bf16[128,2048]{1,0:T(8,128)(2,1)S(1)}, bf16[128,2048]{1,0:T(8,128)(2,1)}, u32[]{:S(2)}) copy-start(bf16[128,2048]{1,0:T(8,128)(2,1)} %param.5) | copy-start | bytes 1572868
  0.0 34.2 %collective-permute-start = (bf16[2048,512]{1,0:T(8,128)(2,1)}, bf16[2048,512]{1,0:T(8,128)(2,1)}, u32[]{:S(2)}, u32[]{:S(2)}) collective-permute-start(bf16[2048,512]{1,0:T(8,128)(2,1)} %bitcast.84), channel_id=1, source_target_pairs={{0,8},{8,0},{16,24},{24,16},{32,40},{40,32},{48,56},{56,48},{64,72... | collective-permute-start | bytes 6291464 | tf_op jit(solution)/shard_map/ppermute | solution.py:16
  2.1 32.2 %collective-permute-start.1 = (bf16[512,2048]{1,0:T(8,128)(2,1)}, bf16[512,2048]{1,0:T(8,128)(2,1)}, u32[]{:S(2)}, u32[]{:S(2)}) collective-permute-start(bf16[512,2048]{1,0:T(8,128)(2,1)} %bitcast.89), channel_id=1, source_target_pairs={{0,8},{8,0},{16,24},{24,16},{32,40},{40,32},{48,56},{56,48},{64,72... | collective-permute-start | bytes 6291464 | tf_op jit(solution)/shard_map/ppermute | solution.py:16
  8.1 26.2 %copy-start = (bf16[1,1,2048,512]{3,2,1,0:T(8,128)(2,1)S(1)}, bf16[1,1,2048,512]{3,2,1,0:T(8,128)(2,1)}, u32[]{:S(2)}) copy-start(bf16[1,1,2048,512]{3,2,1,0:T(8,128)(2,1)} %param.8) | copy-start | bytes 6291460
  39.9 5.0 %copy-start.2 = (f32[2,128,2]{1,2,0:T(2,128)S(1)}, f32[2,128,2]{1,2,0:T(2,128)}, u32[]{:S(2)}) copy-start(f32[2,128,2]{1,2,0:T(2,128)} %param.7) | copy-start | bytes 6148
  39.9 20.8 %all-to-all-start.1 = ((bf16[8,40,2048]{2,1,0:T(8,128)(2,1)}), bf16[8,40,2048]{2,1,0:T(8,128)(2,1)S(1)}, u32[]{:S(2)}, u32[]{:S(2)}) async-start(bf16[8,40,2048]{2,1,0:T(8,128)(2,1)} %bitcast.10), calls=%async_computation.1 | async-start | bytes 2621440 | tf_op jit(solution)/shard_map/all_to_all | solution.py:126
  62.7 20.1 %collective-permute-start.2 = (bf16[128,2048]{1,0:T(8,128)(2,1)S(1)}, bf16[128,2048]{1,0:T(8,128)(2,1)S(1)}, u32[]{:S(2)}, u32[]{:S(2)}) collective-permute-start(bf16[128,2048]{1,0:T(8,128)(2,1)S(1)} %fusion.8), channel_id=1, source_target_pairs={{0,16},{8,24},{16,32},{24,40},{32,48},{40,56},{48,64},{56,72},{64,... | collective-permute-start | bytes 1572872 | tf_op jit(solution)/shard_map/ppermute | solution.py:22
  111.6 20.2 %all-to-all-start.3 = ((bf16[8,40,2048]{2,1,0:T(8,128)(2,1)}), bf16[8,40,2048]{2,1,0:T(8,128)(2,1)S(1)}, u32[]{:S(2)}, u32[]{:S(2)}) async-start(bf16[8,40,2048]{2,1,0:T(8,128)(2,1)} %bitcast.23), calls=%async_computation.3 | async-start | bytes 2621440 | tf_op jit(solution)/shard_map/all_to_all | solution.py:126

commit v6 on v3

--- a/solution.py
+++ b/solution.py
@@ -80,7 +80,8 @@
 
 def slot_tables(ids, groups, slots):
     rows, top = ids.shape
-    flat = ids.reshape(-1)
+    by_choice = ids.T
+    flat = by_choice.reshape(-1)
     count = rows * top
     chosen = (flat[:, None] == jnp.arange(groups, dtype=jnp.int32)[None, :]).astype(jnp.bfloat16)
     earlier = (
@@ -88,9 +89,9 @@
     ).astype(jnp.bfloat16)
     before = jnp.dot(earlier, chosen, preferred_element_type=jnp.float32)
     position = jnp.sum(before * chosen.astype(jnp.float32), axis=1).astype(jnp.int32)
-    position = position.reshape(rows, top)
-    group_hit = ids.T[:, None, None, :] == jnp.arange(groups, dtype=jnp.int32)[None, :, None, None]
-    slot_hit = position.T[:, None, None, :] == jnp.arange(slots, dtype=jnp.int32)[None, None, :, None]
+    position = position.reshape(top, rows)
+    group_hit = by_choice[:, None, None, :] == jnp.arange(groups, dtype=jnp.int32)[None, :, None, None]
+    slot_hit = position[:, None, None, :] == jnp.arange(slots, dtype=jnp.int32)[None, None, :, None]
     return (group_hit & slot_hit).astype(jnp.bfloat16)
 
 

time: 134 us -> 136 us (1.015)
    unnamed x6 -> x8, local copies, waits for them, and re-layouts: 0.02 us -> 1.92 us
where the time goes in v6:
time: 136 us
  waiting for transfers between devices  50.2 us (37%)
  blocking collectives  48.3 us (36%)
  starting transfers between devices  14.8 us (11%)
  Pallas kernels  11.3 us (8%)
  matrix products  6.38 us (5%)
  local copies, waits for them, and re-layouts  2.63 us (2%)
  other arithmetic  1.67 us (1%)
    all_to_all x2, blocking collectives, body(): lax.all_to_all(outgoing, 'expert', split_axis=0, concat_axis=0, tiled=True)  48.3 us
    all_to_all x2, waiting for transfers between devices, body(): lax.all_to_all(expert_out, 'expert', split_axis=0, concat_axis=0, tiled=T...  32.1 us
    ppermute x1, waiting for transfers between devices, shifted(): return lax.ppermute(value, axis, pairs)  18.1 us
    pallas_call x2, Pallas kernels, expert_full(): pl.pallas_call(functools.partial(expert_kernel, block=block), in_specs=[p...  11.3 us
    all_to_all x2, starting transfers between devices, body(): lax.all_to_all(expert_out, 'expert', split_axis=0, concat_axis=0, tiled=T...  8.61 us
    ppermute x2, starting transfers between devices, swapped(): return lax.ppermute(value, axis, pairs)  4.32 us
    dot_general x4, matrix products, body(): jnp.einsum('gsr,gsd->rd', select[k], answers, preferred_element_type=jnp....  3.81 us
  transfers between devices with their start and end apart: 5, of which 3 were waited for; matrix products, arithmetic and copies ran while one was open for 3% of the time, Pallas kernels for 0%

profile of v6, /device:TPU:8, one launch (start us, length us, event | category | flops | bytes accessed | tf_op | source)
XLA Modules:
  0.0 135.5 jit_solution(17291298353383689454)
XLA Ops:
  0.0 1.9 %collective-permute-start = (bf16[2048,512]{1,0:T(8,128)(2,1)}, bf16[2048,512]{1,0:T(8,128)(2,1)S(1)}, u32[]{:S(2)}, u32[]{:S(2)}) collective-permute-start(bf16[2048,512]{1,0:T(8,128)(2,1)} %bitcast.88), channel_id=1, source_target_pairs={{0,8},{8,0},{16,24},{24,16},{32,40},{40,32},{48,56},{56,48},{64,72... | collective-permute-start | bytes 6291464 | tf_op jit(solution)/shard_map/ppermute | solution.py:16
  1.9 2.4 %collective-permute-start.1 = (bf16[512,2048]{1,0:T(8,128)(2,1)}, bf16[512,2048]{1,0:T(8,128)(2,1)S(1)}, u32[]{:S(2)}, u32[]{:S(2)}) collective-permute-start(bf16[512,2048]{1,0:T(8,128)(2,1)} %bitcast.93), channel_id=1, source_target_pairs={{0,8},{8,0},{16,24},{24,16},{32,40},{40,32},{48,56},{56,48},{64,72... | collective-permute-start | bytes 6291464 | tf_op jit(solution)/shard_map/ppermute | solution.py:16
  4.3 0.7 slice_bitcast_fusion.11
  5.0 0.2 fusion.10
  5.3 1.2 fusion.12
  6.6 1.6 %convolution_convert_fusion.1 = bf16[8,40,2048]{2,1,0:T(8,128)(2,1)S(1)} fusion(bf16[8,40,128]{2,1,0:T(8,128)(2,1)S(1)} %convert_reduce_fusion.1, bf16[128,2048]{1,0:T(8,128)(2,1)} %param.5, f32[128]{0:T(128)S(1)} %add_rsqrt_fusion.1), kind=kOutput, calls=%fused_computation.1 | convolution fusion | flops 169213952 | bytes 1917440 | tf_op jit(solution)/shard_map/gsr,rd->gsd/dot_general | solution.py:119
  8.2 0.0 copy-start
  8.2 26.2 %all_to_all.20 = bf16[8,40,2048]{2,1,0:T(8,128)(2,1)S(1)} all-to-all(bf16[8,40,2048]{2,1,0:T(8,128)(2,1)S(1)} %convolution_convert_fusion.1), channel_id=1, replica_groups=mesh['section'=64,'expert'=8] {'expert'}, dimensions={0} | all-to-all | bytes 2621440 | tf_op jit(solution)/shard_map/all_to_all | solution.py:122
  34.3 0.0 collective-permute-done.far_up_hbm
  34.4 0.0 collective-permute-done.1.far_down_hbm
  34.4 0.0 copy-start.2
  34.4 1.3 copy-done.1
  35.7 0.6 copy-done.2
  36.3 0.0 copy-done
  36.3 5.7 %shard_map.55 = bf16[320,2048]{1,0:T(8,128)(2,1)} custom-call(bf16[320,2048]{1,0:T(8,128)(2,1)S(1)} %bitcast.91, bf16[2048,512]{1,0:T(8,128)(2,1)S(1)} %bitcast.89, bf16[512,2048]{1,0:T(8,128)(2,1)} %bitcast.94, bf16[2048,512]{1,0:T(8,128)(2,1)} %copy-done.1, bf16[512,2048]{1,0:T(8,128)(2,1)} %copy-done.2), custom_call_target="tpu_custom_call" | custom-call | flops 2684354560 | bytes 11010048 | tf_op jit(solution)/shard_map/pallas_call | solution.py:64
  41.9 0.0 copy-start.3
  42.0 4.3 %all-to-all-start.1 = ((bf16[8,40,2048]{2,1,0:T(8,128)(2,1)}), bf16[8,40,2048]{2,1,0:T(8,128)(2,1)S(1)}, u32[]{:S(2)}, u32[]{:S(2)}) async-start(bf16[8,40,2048]{2,1,0:T(8,128)(2,1)} %bitcast.12), calls=%async_computation.1 | async-start | bytes 2621440 | tf_op jit(solution)/shard_map/all_to_all | solution.py:126
  46.3 0.0 copy-done.3
  46.3 0.2 fusion.11
  46.6 16.2 %all-to-all-done.1 = bf16[8,40,2048]{2,1,0:T(8,128)(2,1)S(1)} async-done(((bf16[8,40,2048]{2,1,0:T(8,128)(2,1)}), bf16[8,40,2048]{2,1,0:T(8,128)(2,1)S(1)}, u32[]{:S(2)}, u32[]{:S(2)}) %all-to-all-start.1) | async-done | bytes 1310752 | tf_op jit(solution)/shard_map/all_to_all | solution.py:126
  62.8 1.5 %fusion.7 = f32[128,2048]{1,0:T(8,128)S(1)} fusion(bf16[8,40,2048]{2,1,0:T(8,128)(2,1)S(1)} %all-to-all-done.1, bf16[128,2048]{1,0:T(8,128)(2,1)} %param.5, f32[128]{0:T(128)S(1)} %get-tuple-element.16, pred[2,8,40,128]{3,2,1,0:T(8,128)(4,1)S(1)} %broadcast_and_fusion.1), kind=kOutput, calls=%fused_computation.13 | convolution fusion | flops 168558592 | bytes 2925056 | tf_op jit(solution)/shard_map/gsr,gsd->rd/dot_general | solution.py:129
  64.3 0.5 fusion.8
  64.8 1.9 %collective-permute-start.2 = (bf16[128,2048]{1,0:T(8,128)(2,1)S(1)}, bf16[128,2048]{1,0:T(8,128)(2,1)S(1)}, u32[]{:S(2)}, u32[]{:S(2)}) collective-permute-start(bf16[128,2048]{1,0:T(8,128)(2,1)S(1)} %fusion.8), channel_id=1, source_target_pairs={{0,16},{8,24},{16,32},{24,40},{32,48},{40,56},{48,64},{56,72},{64,... | collective-permute-start | bytes 1572872 | tf_op jit(solution)/shard_map/ppermute | solution.py:22
  66.8 18.1 %collective-permute-done.2 = bf16[128,2048]{1,0:T(8,128)(2,1)S(1)} collective-permute-done((bf16[128,2048]{1,0:T(8,128)(2,1)S(1)}, bf16[128,2048]{1,0:T(8,128)(2,1)S(1)}, u32[]{:S(2)}, u32[]{:S(2)}) %collective-permute-start.2) | collective-permute-done | bytes 524320 | tf_op jit(solution)/shard_map/ppermute | solution.py:22
  84.9 0.2 fusion.14
  85.1 0.6 convolution_convert_fusion
  85.7 22.2 %all_to_all.21 = bf16[8,40,2048]{2,1,0:T(8,128)(2,1)S(1)} all-to-all(bf16[8,40,2048]{2,1,0:T(8,128)(2,1)S(1)} %convolution_convert_fusion), channel_id=1, replica_groups=mesh['section'=64,'expert'=8] {'expert'}, dimensions={0} | all-to-all | bytes 2621440 | tf_op jit(solution)/shard_map/all_to_all | solution.py:122
  107.8 5.7 %shard_map.56 = bf16[320,2048]{1,0:T(8,128)(2,1)} custom-call(bf16[320,2048]{1,0:T(8,128)(2,1)S(1)} %bitcast.92, bf16[2048,512]{1,0:T(8,128)(2,1)S(1)} %bitcast.90, bf16[512,2048]{1,0:T(8,128)(2,1)} %bitcast.95, bf16[2048,512]{1,0:T(8,128)(2,1)} %copy-done.1, bf16[512,2048]{1,0:T(8,128)(2,1)} %copy-done.2), custom_call_target="tpu_custom_call" | custom-call | flops 2684354560 | bytes 11010048 | tf_op jit(solution)/shard_map/pallas_call | solution.py:64
  113.5 4.3 %all-to-all-start.3 = ((bf16[8,40,2048]{2,1,0:T(8,128)(2,1)}), bf16[8,40,2048]{2,1,0:T(8,128)(2,1)S(1)}, u32[]{:S(2)}, u32[]{:S(2)}) async-start(bf16[8,40,2048]{2,1,0:T(8,128)(2,1)} %bitcast.27), calls=%async_computation.3 | async-start | bytes 2621440 | tf_op jit(solution)/shard_map/all_to_all | solution.py:126
  117.8 15.9 %all-to-all-done.3 = bf16[8,40,2048]{2,1,0:T(8,128)(2,1)S(1)} async-done(((bf16[8,40,2048]{2,1,0:T(8,128)(2,1)}), bf16[8,40,2048]{2,1,0:T(8,128)(2,1)S(1)}, u32[]{:S(2)}, u32[]{:S(2)}) %all-to-all-start.3) | async-done | bytes 1310752 | tf_op jit(solution)/shard_map/all_to_all | solution.py:126
  133.7 0.5 fusion
  134.2 1.3 fusion.9
  (17 shorter events, 0.3 us)
Async XLA Ops:
  0.0 34.4 %collective-permute-start = (bf16[2048,512]{1,0:T(8,128)(2,1)}, bf16[2048,512]{1,0:T(8,128)(2,1)S(1)}, u32[]{:S(2)}, u32[]{:S(2)}) collective-permute-start(bf16[2048,512]{1,0:T(8,128)(2,1)} %bitcast.88), channel_id=1, source_target_pairs={{0,8},{8,0},{16,24},{24,16},{32,40},{40,32},{48,56},{56,48},{64,72... | collective-permute-start | bytes 6291464 | tf_op jit(solution)/shard_map/ppermute | solution.py:16
  1.9 32.4 %collective-permute-start.1 = (bf16[512,2048]{1,0:T(8,128)(2,1)}, bf16[512,2048]{1,0:T(8,128)(2,1)S(1)}, u32[]{:S(2)}, u32[]{:S(2)}) collective-permute-start(bf16[512,2048]{1,0:T(8,128)(2,1)} %bitcast.93), channel_id=1, source_target_pairs={{0,8},{8,0},{16,24},{24,16},{32,40},{40,32},{48,56},{56,48},{64,72... | collective-permute-start | bytes 6291464 | tf_op jit(solution)/shard_map/ppermute | solution.py:16
  8.2 28.1 %copy-start = (bf16[1,1,2048,512]{3,2,1,0:T(8,128)(2,1)S(1)}, bf16[1,1,2048,512]{3,2,1,0:T(8,128)(2,1)}, u32[]{:S(2)}) copy-start(bf16[1,1,2048,512]{3,2,1,0:T(8,128)(2,1)} %param.8) | copy-start | bytes 6291460
  34.4 1.4 copy-start.1
  34.4 1.9 %copy-start.2 = (bf16[512,2048]{1,0:T(8,128)(2,1)}, bf16[512,2048]{1,0:T(8,128)(2,1)S(1)}, u32[]{:S(2)}) copy-start(bf16[512,2048]{1,0:T(8,128)(2,1)S(1)} %collective-permute-done.1.far_down_hbm) | copy-start | bytes 6291460
  41.9 4.3 %copy-start.3 = (f32[2,128,2]{1,2,0:T(2,128)S(1)}, f32[2,128,2]{1,2,0:T(2,128)}, u32[]{:S(2)}) copy-start(f32[2,128,2]{1,2,0:T(2,128)} %param.7) | copy-start | bytes 6148
  42.0 20.8 %all-to-all-start.1 = ((bf16[8,40,2048]{2,1,0:T(8,128)(2,1)}), bf16[8,40,2048]{2,1,0:T(8,128)(2,1)S(1)}, u32[]{:S(2)}, u32[]{:S(2)}) async-start(bf16[8,40,2048]{2,1,0:T(8,128)(2,1)} %bitcast.12), calls=%async_computation.1 | async-start | bytes 2621440 | tf_op jit(solution)/shard_map/all_to_all | solution.py:126
  64.8 20.1 %collective-permute-start.2 = (bf16[128,2048]{1,0:T(8,128)(2,1)S(1)}, bf16[128,2048]{1,0:T(8,128)(2,1)S(1)}, u32[]{:S(2)}, u32[]{:S(2)}) collective-permute-start(bf16[128,2048]{1,0:T(8,128)(2,1)S(1)} %fusion.8), channel_id=1, source_target_pairs={{0,16},{8,24},{16,32},{24,40},{32,48},{40,56},{48,64},{56,72},{64,... | collective-permute-start | bytes 1572872 | tf_op jit(solution)/shard_map/ppermute | solution.py:22
  113.5 20.2 %all-to-all-start.3 = ((bf16[8,40,2048]{2,1,0:T(8,128)(2,1)}), bf16[8,40,2048]{2,1,0:T(8,128)(2,1)S(1)}, u32[]{:S(2)}, u32[]{:S(2)}) async-start(bf16[8,40,2048]{2,1,0:T(8,128)(2,1)} %bitcast.27), calls=%async_computation.3 | async-start | bytes 2621440 | tf_op jit(solution)/shard_map/all_to_all | solution.py:126

commit v7 on v3

--- a/solution.py
+++ b/solution.py
@@ -102,7 +102,6 @@
     slots = -(-slots // 8) * 8
     up_local = up_weight.reshape(up_weight.shape[2], up_weight.shape[3])
     down_local = down_weight.reshape(down_weight.shape[2], down_weight.shape[3])
-    partner_up, partner_down = swapped((up_local, down_local), "section", 0)
     state = tokens
     for tick in range(TICKS):
         if tick > 0:
@@ -118,6 +117,11 @@
         outgoing = jnp.einsum(
             "gsr,rd->gsd", dispatch, normed, preferred_element_type=jnp.float32
         ).astype(jnp.bfloat16)
+        if tick == 0:
+            outgoing, up_local, down_local = lax.optimization_barrier(
+                (outgoing, up_local, down_local)
+            )
+            partner_up, partner_down = swapped((up_local, down_local), "section", 0)
         received = lax.all_to_all(outgoing, "expert", split_axis=0, concat_axis=0, tiled=True)
         expert_out = expert_full(
             received.reshape(groups * slots, -1), up_local, down_local, partner_up, partner_down

time: 134 us -> 135 us (level)
  local copies, waits for them, and re-layouts: 1.61 us -> 3.58 us
    unnamed x6 -> x10, local copies, waits for them, and re-layouts: 0.02 us -> 1.93 us
  transfers between devices with their start and end apart: 5 -> 5, of which waited for: 3 -> 3; matrix products, arithmetic and copies ran while one was open for 3% -> 1% of each run, Pallas kernels for 0% -> 0%
where the time goes in v7:
time: 135 us
  waiting for transfers between devices  49.7 us (37%)
  blocking collectives  48.2 us (36%)
  starting transfers between devices  14.9 us (11%)
  Pallas kernels  11.3 us (8%)
  matrix products  5.34 us (4%)
  local copies, waits for them, and re-layouts  3.58 us (3%)
  other arithmetic  1.82 us (1%)
    all_to_all x2, blocking collectives, body(): lax.all_to_all(outgoing, 'expert', split_axis=0, concat_axis=0, tiled=True)  48.2 us
    all_to_all x2, waiting for transfers between devices, body(): lax.all_to_all(expert_out, 'expert', split_axis=0, concat_axis=0, tiled=T...  31.6 us
    ppermute x1, waiting for transfers between devices, shifted(): return lax.ppermute(value, axis, pairs)  18.1 us
    pallas_call x2, Pallas kernels, expert_full(): pl.pallas_call(functools.partial(expert_kernel, block=block), in_specs=[p...  11.3 us
    all_to_all x2, starting transfers between devices, body(): lax.all_to_all(expert_out, 'expert', split_axis=0, concat_axis=0, tiled=T...  8.61 us
    ppermute x2, starting transfers between devices, swapped(): return lax.ppermute(value, axis, pairs)  4.33 us
    dot_general x4, matrix products, body(): jnp.einsum('gsr,gsd->rd', select[k], answers, preferred_element_type=jnp....  3.8 us
  transfers between devices with their start and end apart: 5, of which 3 were waited for; matrix products, arithmetic and copies ran while one was open for 1% of the time, Pallas kernels for 0%

profile of v7, /device:TPU:8, one launch (start us, length us, event | category | flops | bytes accessed | tf_op | source)
XLA Modules:
  0.0 135.0 jit_solution(908189594031575213)
XLA Ops:
  0.0 0.8 slice_bitcast_fusion.13
  0.8 0.1 copy.6
  0.9 0.1 eq.105
  1.0 0.2 fusion.10
  1.2 0.1 convert_element_type.66
  1.4 0.1 copy.7
  1.5 1.4 %fusion.12 = f32[128]{0:T(128)S(1)} fusion(bf16[128,2048]{1,0:T(8,128)(2,1)} %param.5), kind=kLoop, calls=%fused_computation.24 | loop fusion | flops 786304 | bytes 524800 | tf_op jit(solution)/shard_map/reduce_sum | solution.py:113
  2.9 0.6 convolution_convert_fusion.1
  3.5 1.9 %collective-permute-start = (bf16[2048,512]{1,0:T(8,128)(2,1)S(1)}, bf16[2048,512]{1,0:T(8,128)(2,1)S(1)}, u32[]{:S(2)}, u32[]{:S(2)}) collective-permute-start(bf16[2048,512]{1,0:T(8,128)(2,1)S(1)} %bitcast.80), channel_id=1, source_target_pairs={{0,8},{8,0},{16,24},{24,16},{32,40},{40,32},{48,56},{56,48},{64,72... | collective-permute-start | bytes 6291464 | tf_op jit(solution)/shard_map/ppermute | solution.py:16
  5.4 2.4 %collective-permute-start.1 = (bf16[512,2048]{1,0:T(8,128)(2,1)}, bf16[512,2048]{1,0:T(8,128)(2,1)S(1)}, u32[]{:S(2)}, u32[]{:S(2)}) collective-permute-start(bf16[512,2048]{1,0:T(8,128)(2,1)} %bitcast.85), channel_id=1, source_target_pairs={{0,8},{8,0},{16,24},{24,16},{32,40},{40,32},{48,56},{56,48},{64,72... | collective-permute-start | bytes 6291464 | tf_op jit(solution)/shard_map/ppermute | solution.py:16
  7.8 26.0 %all_to_all.20 = bf16[8,40,2048]{2,1,0:T(8,128)(2,1)S(1)} all-to-all(bf16[8,40,2048]{2,1,0:T(8,128)(2,1)S(1)} %convolution_convert_fusion.1), channel_id=1, replica_groups=mesh['section'=64,'expert'=8] {'expert'}, dimensions={0} | all-to-all | bytes 2621440 | tf_op jit(solution)/shard_map/all_to_all | solution.py:125
  33.9 1.3 copy-done.1
  35.2 0.6 copy-done.2
  35.8 5.7 %shard_map.55 = bf16[320,2048]{1,0:T(8,128)(2,1)} custom-call(bf16[320,2048]{1,0:T(8,128)(2,1)S(1)} %bitcast.83, bf16[2048,512]{1,0:T(8,128)(2,1)S(1)} %bitcast.81, bf16[512,2048]{1,0:T(8,128)(2,1)} %bitcast.86, bf16[2048,512]{1,0:T(8,128)(2,1)} %copy-done.1, bf16[512,2048]{1,0:T(8,128)(2,1)} %copy-done.2), custom_call_target="tpu_custom_call" | custom-call | flops 2684354560 | bytes 11010048 | tf_op jit(solution)/shard_map/pallas_call | solution.py:64
  41.5 4.3 %all-to-all-start.1 = ((bf16[8,40,2048]{2,1,0:T(8,128)(2,1)}), bf16[8,40,2048]{2,1,0:T(8,128)(2,1)S(1)}, u32[]{:S(2)}, u32[]{:S(2)}) async-start(bf16[8,40,2048]{2,1,0:T(8,128)(2,1)} %bitcast.10), calls=%async_computation.1 | async-start | bytes 2621440 | tf_op jit(solution)/shard_map/all_to_all | solution.py:129
  45.8 0.1 copy.8
  45.9 0.1 eq.115
  46.0 0.2 fusion.11
  46.2 0.1 convert_element_type.75
  46.6 15.7 %all-to-all-done.1 = bf16[8,40,2048]{2,1,0:T(8,128)(2,1)S(1)} async-done(((bf16[8,40,2048]{2,1,0:T(8,128)(2,1)}), bf16[8,40,2048]{2,1,0:T(8,128)(2,1)S(1)}, u32[]{:S(2)}, u32[]{:S(2)}) %all-to-all-start.1) | async-done | bytes 1310752 | tf_op jit(solution)/shard_map/all_to_all | solution.py:129
  62.3 1.5 %fusion.7 = f32[128,2048]{1,0:T(8,128)S(1)} fusion(bf16[8,40,2048]{2,1,0:T(8,128)(2,1)S(1)} %all-to-all-done.1, bf16[128,2048]{1,0:T(8,128)(2,1)} %param.5, f32[128]{0:T(128)S(1)} %get-tuple-element.22, pred[2,8,40,128]{3,2,1,0:T(8,128)(4,1)S(1)} %broadcast_and_fusion.1), kind=kOutput, calls=%fused_computation.13 | convolution fusion | flops 168558592 | bytes 2925056 | tf_op jit(solution)/shard_map/gsr,gsd->rd/dot_general | solution.py:132
  63.8 0.5 fusion.8
  64.3 1.9 %collective-permute-start.2 = (bf16[128,2048]{1,0:T(8,128)(2,1)S(1)}, bf16[128,2048]{1,0:T(8,128)(2,1)S(1)}, u32[]{:S(2)}, u32[]{:S(2)}) collective-permute-start(bf16[128,2048]{1,0:T(8,128)(2,1)S(1)} %fusion.8), channel_id=1, source_target_pairs={{0,16},{8,24},{16,32},{24,40},{32,48},{40,56},{48,64},{56,72},{64,... | collective-permute-start | bytes 1572872 | tf_op jit(solution)/shard_map/ppermute | solution.py:22
  66.3 18.1 %collective-permute-done.2 = bf16[128,2048]{1,0:T(8,128)(2,1)S(1)} collective-permute-done((bf16[128,2048]{1,0:T(8,128)(2,1)S(1)}, bf16[128,2048]{1,0:T(8,128)(2,1)S(1)}, u32[]{:S(2)}, u32[]{:S(2)}) %collective-permute-start.2) | collective-permute-done | bytes 524320 | tf_op jit(solution)/shard_map/ppermute | solution.py:22
  84.4 0.2 fusion.14
  84.6 0.6 convolution_convert_fusion
  85.2 22.2 %all_to_all.21 = bf16[8,40,2048]{2,1,0:T(8,128)(2,1)S(1)} all-to-all(bf16[8,40,2048]{2,1,0:T(8,128)(2,1)S(1)} %convolution_convert_fusion), channel_id=1, replica_groups=mesh['section'=64,'expert'=8] {'expert'}, dimensions={0} | all-to-all | bytes 2621440 | tf_op jit(solution)/shard_map/all_to_all | solution.py:125
  107.3 5.7 %shard_map.56 = bf16[320,2048]{1,0:T(8,128)(2,1)} custom-call(bf16[320,2048]{1,0:T(8,128)(2,1)S(1)} %bitcast.84, bf16[2048,512]{1,0:T(8,128)(2,1)S(1)} %bitcast.82, bf16[512,2048]{1,0:T(8,128)(2,1)} %bitcast.87, bf16[2048,512]{1,0:T(8,128)(2,1)} %copy-done.1, bf16[512,2048]{1,0:T(8,128)(2,1)} %copy-done.2), custom_call_target="tpu_custom_call" | custom-call | flops 2684354560 | bytes 11010048 | tf_op jit(solution)/shard_map/pallas_call | solution.py:64
  113.0 4.3 %all-to-all-start.3 = ((bf16[8,40,2048]{2,1,0:T(8,128)(2,1)}), bf16[8,40,2048]{2,1,0:T(8,128)(2,1)S(1)}, u32[]{:S(2)}, u32[]{:S(2)}) async-start(bf16[8,40,2048]{2,1,0:T(8,128)(2,1)} %bitcast.23), calls=%async_computation.3 | async-start | bytes 2621440 | tf_op jit(solution)/shard_map/all_to_all | solution.py:129
  117.3 15.9 %all-to-all-done.3 = bf16[8,40,2048]{2,1,0:T(8,128)(2,1)S(1)} async-done(((bf16[8,40,2048]{2,1,0:T(8,128)(2,1)}), bf16[8,40,2048]{2,1,0:T(8,128)(2,1)S(1)}, u32[]{:S(2)}, u32[]{:S(2)}) %all-to-all-start.3) | async-done | bytes 1310752 | tf_op jit(solution)/shard_map/all_to_all | solution.py:129
  133.2 0.5 fusion
  133.7 1.3 fusion.9
  (27 shorter events, 0.4 us)
Async XLA Ops:
  0.0 2.9 %copy-start.3 = (bf16[128,2048]{1,0:T(8,128)(2,1)S(1)}, bf16[128,2048]{1,0:T(8,128)(2,1)}, u32[]{:S(2)}) copy-start(bf16[128,2048]{1,0:T(8,128)(2,1)} %param.5) | copy-start | bytes 1572868
  1.4 2.1 %copy-start = (bf16[1,1,2048,512]{3,2,1,0:T(8,128)(2,1)S(1)}, bf16[1,1,2048,512]{3,2,1,0:T(8,128)(2,1)}, u32[]{:S(2)}) copy-start(bf16[1,1,2048,512]{3,2,1,0:T(8,128)(2,1)} %param.8) | copy-start | bytes 6291460
  3.5 30.4 %collective-permute-start = (bf16[2048,512]{1,0:T(8,128)(2,1)S(1)}, bf16[2048,512]{1,0:T(8,128)(2,1)S(1)}, u32[]{:S(2)}, u32[]{:S(2)}) collective-permute-start(bf16[2048,512]{1,0:T(8,128)(2,1)S(1)} %bitcast.80), channel_id=1, source_target_pairs={{0,8},{8,0},{16,24},{24,16},{32,40},{40,32},{48,56},{56,48},{64,72... | collective-permute-start | bytes 6291464 | tf_op jit(solution)/shard_map/ppermute | solution.py:16
  5.4 28.4 %collective-permute-start.1 = (bf16[512,2048]{1,0:T(8,128)(2,1)}, bf16[512,2048]{1,0:T(8,128)(2,1)S(1)}, u32[]{:S(2)}, u32[]{:S(2)}) collective-permute-start(bf16[512,2048]{1,0:T(8,128)(2,1)} %bitcast.85), channel_id=1, source_target_pairs={{0,8},{8,0},{16,24},{24,16},{32,40},{40,32},{48,56},{56,48},{64,72... | collective-permute-start | bytes 6291464 | tf_op jit(solution)/shard_map/ppermute | solution.py:16
  33.9 1.4 %copy-start.1 = (bf16[2048,512]{1,0:T(8,128)(2,1)}, bf16[2048,512]{1,0:T(8,128)(2,1)S(1)}, u32[]{:S(2)}) copy-start(bf16[2048,512]{1,0:T(8,128)(2,1)S(1)} %collective-permute-done.far_up_hbm) | copy-start | bytes 6291460
  33.9 1.9 %copy-start.2 = (bf16[512,2048]{1,0:T(8,128)(2,1)}, bf16[512,2048]{1,0:T(8,128)(2,1)S(1)}, u32[]{:S(2)}) copy-start(bf16[512,2048]{1,0:T(8,128)(2,1)S(1)} %collective-permute-done.1.far_down_hbm) | copy-start | bytes 6291460
  41.5 5.0 %copy-start.4 = (f32[2,128,2]{1,2,0:T(2,128)S(1)}, f32[2,128,2]{1,2,0:T(2,128)}, u32[]{:S(2)}) copy-start(f32[2,128,2]{1,2,0:T(2,128)} %param.7) | copy-start | bytes 6148
  41.5 20.8 %all-to-all-start.1 = ((bf16[8,40,2048]{2,1,0:T(8,128)(2,1)}), bf16[8,40,2048]{2,1,0:T(8,128)(2,1)S(1)}, u32[]{:S(2)}, u32[]{:S(2)}) async-start(bf16[8,40,2048]{2,1,0:T(8,128)(2,1)} %bitcast.10), calls=%async_computation.1 | async-start | bytes 2621440 | tf_op jit(solution)/shard_map/all_to_all | solution.py:129
  64.3 20.1 %collective-permute-start.2 = (bf16[128,2048]{1,0:T(8,128)(2,1)S(1)}, bf16[128,2048]{1,0:T(8,128)(2,1)S(1)}, u32[]{:S(2)}, u32[]{:S(2)}) collective-permute-start(bf16[128,2048]{1,0:T(8,128)(2,1)S(1)} %fusion.8), channel_id=1, source_target_pairs={{0,16},{8,24},{16,32},{24,40},{32,48},{40,56},{48,64},{56,72},{64,... | collective-permute-start | bytes 1572872 | tf_op jit(solution)/shard_map/ppermute | solution.py:22
  113.0 20.2 %all-to-all-start.3 = ((bf16[8,40,2048]{2,1,0:T(8,128)(2,1)}), bf16[8,40,2048]{2,1,0:T(8,128)(2,1)S(1)}, u32[]{:S(2)}, u32[]{:S(2)}) async-start(bf16[8,40,2048]{2,1,0:T(8,128)(2,1)} %bitcast.23), calls=%async_computation.3 | async-start | bytes 2621440 | tf_op jit(solution)/shard_map/all_to_all | solution.py:129

commit v8 on v3

--- a/solution.py
+++ b/solution.py
@@ -73,7 +73,7 @@
             pltpu.VMEM(far_down.shape, far_down.dtype),
             pltpu.SemaphoreType.DMA((4,)),
         ],
-        compiler_params=pltpu.CompilerParams(vmem_limit_bytes=48 * 1024 * 1024),
+        compiler_params=pltpu.CompilerParams(vmem_limit_bytes=24 * 1024 * 1024),
         cost_estimate=cost,
     )(rows, own_up, own_down, far_up, far_down)
 

time: 134 us -> 133 us (level)
  no operation moved by 1% of the time
where the time goes in v8:
time: 133 us
  waiting for transfers between devices  49.7 us (37%)
  blocking collectives  48.4 us (36%)
  starting transfers between devices  15 us (11%)
  Pallas kernels  10.7 us (8%)
  matrix products  5.35 us (4%)
  other arithmetic  1.69 us (1%)
  local copies, waits for them, and re-layouts  1.63 us (1%)
    all_to_all x2, blocking collectives, body(): lax.all_to_all(outgoing, 'expert', split_axis=0, concat_axis=0, tiled=True)  48.4 us
    all_to_all x2, waiting for transfers between devices, body(): lax.all_to_all(expert_out, 'expert', split_axis=0, concat_axis=0, tiled=T...  31.6 us
    ppermute x1, waiting for transfers between devices, shifted(): return lax.ppermute(value, axis, pairs)  18.1 us
    pallas_call x2, Pallas kernels, expert_full(): pl.pallas_call(functools.partial(expert_kernel, block=block), in_specs=[p...  10.7 us
    all_to_all x2, starting transfers between devices, body(): lax.all_to_all(expert_out, 'expert', split_axis=0, concat_axis=0, tiled=T...  8.61 us
    ppermute x2, starting transfers between devices, swapped(): return lax.ppermute(value, axis, pairs)  4.45 us
    dot_general x4, matrix products, body(): jnp.einsum('gsr,gsd->rd', select[k], answers, preferred_element_type=jnp....  3.81 us
  transfers between devices with their start and end apart: 5, of which 3 were waited for; matrix products, arithmetic and copies ran while one was open for 3% of the time, Pallas kernels for 0%

profile of v8, /device:TPU:8, one launch (start us, length us, event | category | flops | bytes accessed | tf_op | source)
XLA Modules:
  0.0 132.8 jit_solution(8394352959157391862)
XLA Ops:
  0.0 2.0 %collective-permute-start = (bf16[2048,512]{1,0:T(8,128)(2,1)}, bf16[2048,512]{1,0:T(8,128)(2,1)}, u32[]{:S(2)}, u32[]{:S(2)}) collective-permute-start(bf16[2048,512]{1,0:T(8,128)(2,1)} %bitcast.80), channel_id=1, source_target_pairs={{0,8},{8,0},{16,24},{24,16},{32,40},{40,32},{48,56},{56,48},{64,72... | collective-permute-start | bytes 6291464 | tf_op jit(solution)/shard_map/ppermute | solution.py:16
  2.1 2.4 %collective-permute-start.1 = (bf16[512,2048]{1,0:T(8,128)(2,1)}, bf16[512,2048]{1,0:T(8,128)(2,1)}, u32[]{:S(2)}, u32[]{:S(2)}) collective-permute-start(bf16[512,2048]{1,0:T(8,128)(2,1)} %bitcast.83), channel_id=1, source_target_pairs={{0,8},{8,0},{16,24},{24,16},{32,40},{40,32},{48,56},{56,48},{64,72... | collective-permute-start | bytes 6291464 | tf_op jit(solution)/shard_map/ppermute | solution.py:16
  4.5 0.7 slice_bitcast_fusion.13
  5.2 0.1 copy.6
  5.3 0.1 eq.105
  5.4 0.2 fusion.10
  5.6 0.1 convert_element_type.66
  5.8 0.1 copy.7
  5.9 1.2 fusion.12
  7.2 0.0 copy-start.1
  7.2 0.6 convolution_convert_fusion.1
  7.8 26.1 %all_to_all.20 = bf16[8,40,2048]{2,1,0:T(8,128)(2,1)S(1)} all-to-all(bf16[8,40,2048]{2,1,0:T(8,128)(2,1)S(1)} %convolution_convert_fusion.1), channel_id=1, replica_groups=mesh['section'=64,'expert'=8] {'expert'}, dimensions={0} | all-to-all | bytes 2621440 | tf_op jit(solution)/shard_map/all_to_all | solution.py:121
  34.0 5.4 %shard_map.55 = bf16[320,2048]{1,0:T(8,128)(2,1)} custom-call(bf16[320,2048]{1,0:T(8,128)(2,1)S(1)} %bitcast.86, bf16[2048,512]{1,0:T(8,128)(2,1)S(1)} %bitcast.81, bf16[512,2048]{1,0:T(8,128)(2,1)S(1)} %bitcast.84, bf16[2048,512]{1,0:T(8,128)(2,1)} %collective-permute-done.far_up_hbm, bf16[512,2048]{1,0:T(8,128)(2,1)} %collective-permute-done.1.far_down_hbm), custom_call_target="tpu_custom_call" | custom-call | flops 2684354560 | bytes 11010048 | tf_op jit(solution)/shard_map/pallas_call | solution.py:64
  39.3 4.3 %all-to-all-start.1 = ((bf16[8,40,2048]{2,1,0:T(8,128)(2,1)}), bf16[8,40,2048]{2,1,0:T(8,128)(2,1)S(1)}, u32[]{:S(2)}, u32[]{:S(2)}) async-start(bf16[8,40,2048]{2,1,0:T(8,128)(2,1)} %bitcast.10), calls=%async_computation.1 | async-start | bytes 2621440 | tf_op jit(solution)/shard_map/all_to_all | solution.py:125
  43.6 0.1 copy.8
  43.8 0.1 eq.115
  43.9 0.2 fusion.11
  44.1 0.1 convert_element_type.75
  44.3 0.1 copy.9
  44.4 15.7 %all-to-all-done.1 = bf16[8,40,2048]{2,1,0:T(8,128)(2,1)S(1)} async-done(((bf16[8,40,2048]{2,1,0:T(8,128)(2,1)}), bf16[8,40,2048]{2,1,0:T(8,128)(2,1)S(1)}, u32[]{:S(2)}, u32[]{:S(2)}) %all-to-all-start.1) | async-done | bytes 1310752 | tf_op jit(solution)/shard_map/all_to_all | solution.py:125
  60.1 1.5 %fusion.7 = f32[128,2048]{1,0:T(8,128)S(1)} fusion(bf16[8,40,2048]{2,1,0:T(8,128)(2,1)S(1)} %all-to-all-done.1, bf16[128,2048]{1,0:T(8,128)(2,1)} %param.5, f32[128]{0:T(128)S(1)} %get-tuple-element.16, pred[2,8,40,128]{3,2,1,0:T(8,128)(4,1)S(1)} %broadcast_and_fusion.1), kind=kOutput, calls=%fused_computation.13 | convolution fusion | flops 168558592 | bytes 2925056 | tf_op jit(solution)/shard_map/gsr,gsd->rd/dot_general | solution.py:128
  61.7 0.5 fusion.8
  62.2 1.9 %collective-permute-start.2 = (bf16[128,2048]{1,0:T(8,128)(2,1)S(1)}, bf16[128,2048]{1,0:T(8,128)(2,1)S(1)}, u32[]{:S(2)}, u32[]{:S(2)}) collective-permute-start(bf16[128,2048]{1,0:T(8,128)(2,1)S(1)} %fusion.8), channel_id=1, source_target_pairs={{0,16},{8,24},{16,32},{24,40},{32,48},{40,56},{48,64},{56,72},{64,... | collective-permute-start | bytes 1572872 | tf_op jit(solution)/shard_map/ppermute | solution.py:22
  64.2 18.1 %collective-permute-done.2 = bf16[128,2048]{1,0:T(8,128)(2,1)S(1)} collective-permute-done((bf16[128,2048]{1,0:T(8,128)(2,1)S(1)}, bf16[128,2048]{1,0:T(8,128)(2,1)S(1)}, u32[]{:S(2)}, u32[]{:S(2)}) %collective-permute-start.2) | collective-permute-done | bytes 524320 | tf_op jit(solution)/shard_map/ppermute | solution.py:22
  82.2 0.2 fusion.14
  82.4 0.6 convolution_convert_fusion
  83.0 22.3 %all_to_all.21 = bf16[8,40,2048]{2,1,0:T(8,128)(2,1)S(1)} all-to-all(bf16[8,40,2048]{2,1,0:T(8,128)(2,1)S(1)} %convolution_convert_fusion), channel_id=1, replica_groups=mesh['section'=64,'expert'=8] {'expert'}, dimensions={0} | all-to-all | bytes 2621440 | tf_op jit(solution)/shard_map/all_to_all | solution.py:121
  105.3 5.4 %shard_map.56 = bf16[320,2048]{1,0:T(8,128)(2,1)} custom-call(bf16[320,2048]{1,0:T(8,128)(2,1)S(1)} %bitcast.87, bf16[2048,512]{1,0:T(8,128)(2,1)S(1)} %bitcast.82, bf16[512,2048]{1,0:T(8,128)(2,1)S(1)} %bitcast.85, bf16[2048,512]{1,0:T(8,128)(2,1)} %collective-permute-done.far_up_hbm, bf16[512,2048]{1,0:T(8,128)(2,1)} %collective-permute-done.1.far_down_hbm), custom_call_target="tpu_custom_call" | custom-call | flops 2684354560 | bytes 11010048 | tf_op jit(solution)/shard_map/pallas_call | solution.py:64
  110.7 4.3 %all-to-all-start.3 = ((bf16[8,40,2048]{2,1,0:T(8,128)(2,1)}), bf16[8,40,2048]{2,1,0:T(8,128)(2,1)S(1)}, u32[]{:S(2)}, u32[]{:S(2)}) async-start(bf16[8,40,2048]{2,1,0:T(8,128)(2,1)} %bitcast.23), calls=%async_computation.3 | async-start | bytes 2621440 | tf_op jit(solution)/shard_map/all_to_all | solution.py:125
  115.1 15.9 %all-to-all-done.3 = bf16[8,40,2048]{2,1,0:T(8,128)(2,1)S(1)} async-done(((bf16[8,40,2048]{2,1,0:T(8,128)(2,1)}), bf16[8,40,2048]{2,1,0:T(8,128)(2,1)S(1)}, u32[]{:S(2)}, u32[]{:S(2)}) %all-to-all-start.3) | async-done | bytes 1310752 | tf_op jit(solution)/shard_map/all_to_all | solution.py:125
  131.0 0.5 fusion
  131.4 1.3 fusion.9
  (27 shorter events, 0.3 us)
Async XLA Ops:
  0.0 7.2 %copy-start.3 = (bf16[128,2048]{1,0:T(8,128)(2,1)S(1)}, bf16[128,2048]{1,0:T(8,128)(2,1)}, u32[]{:S(2)}) copy-start(bf16[128,2048]{1,0:T(8,128)(2,1)} %param.5) | copy-start | bytes 1572868
  0.0 33.9 %collective-permute-start = (bf16[2048,512]{1,0:T(8,128)(2,1)}, bf16[2048,512]{1,0:T(8,128)(2,1)}, u32[]{:S(2)}, u32[]{:S(2)}) collective-permute-start(bf16[2048,512]{1,0:T(8,128)(2,1)} %bitcast.80), channel_id=1, source_target_pairs={{0,8},{8,0},{16,24},{24,16},{32,40},{40,32},{48,56},{56,48},{64,72... | collective-permute-start | bytes 6291464 | tf_op jit(solution)/shard_map/ppermute | solution.py:16
  2.1 31.9 %collective-permute-start.1 = (bf16[512,2048]{1,0:T(8,128)(2,1)}, bf16[512,2048]{1,0:T(8,128)(2,1)}, u32[]{:S(2)}, u32[]{:S(2)}) collective-permute-start(bf16[512,2048]{1,0:T(8,128)(2,1)} %bitcast.83), channel_id=1, source_target_pairs={{0,8},{8,0},{16,24},{24,16},{32,40},{40,32},{48,56},{56,48},{64,72... | collective-permute-start | bytes 6291464 | tf_op jit(solution)/shard_map/ppermute | solution.py:16
  7.2 26.8 %copy-start.1 = (bf16[1,1,512,2048]{3,2,1,0:T(8,128)(2,1)S(1)}, bf16[1,1,512,2048]{3,2,1,0:T(8,128)(2,1)}, u32[]{:S(2)}) copy-start(bf16[1,1,512,2048]{3,2,1,0:T(8,128)(2,1)} %param.9) | copy-start | bytes 6291460
  7.8 26.2 %copy-start = (bf16[1,1,2048,512]{3,2,1,0:T(8,128)(2,1)S(1)}, bf16[1,1,2048,512]{3,2,1,0:T(8,128)(2,1)}, u32[]{:S(2)}) copy-start(bf16[1,1,2048,512]{3,2,1,0:T(8,128)(2,1)} %param.8) | copy-start | bytes 6291460
  39.3 5.0 %copy-start.4 = (f32[2,128,2]{1,2,0:T(2,128)S(1)}, f32[2,128,2]{1,2,0:T(2,128)}, u32[]{:S(2)}) copy-start(f32[2,128,2]{1,2,0:T(2,128)} %param.7) | copy-start | bytes 6148
  39.3 20.8 %all-to-all-start.1 = ((bf16[8,40,2048]{2,1,0:T(8,128)(2,1)}), bf16[8,40,2048]{2,1,0:T(8,128)(2,1)S(1)}, u32[]{:S(2)}, u32[]{:S(2)}) async-start(bf16[8,40,2048]{2,1,0:T(8,128)(2,1)} %bitcast.10), calls=%async_computation.1 | async-start | bytes 2621440 | tf_op jit(solution)/shard_map/all_to_all | solution.py:125
  62.2 20.1 %collective-permute-start.2 = (bf16[128,2048]{1,0:T(8,128)(2,1)S(1)}, bf16[128,2048]{1,0:T(8,128)(2,1)S(1)}, u32[]{:S(2)}, u32[]{:S(2)}) collective-permute-start(bf16[128,2048]{1,0:T(8,128)(2,1)S(1)} %fusion.8), channel_id=1, source_target_pairs={{0,16},{8,24},{16,32},{24,40},{32,48},{40,56},{48,64},{56,72},{64,... | collective-permute-start | bytes 1572872 | tf_op jit(solution)/shard_map/ppermute | solution.py:22
  83.0 22.3 %copy-start.2 = (bf16[1,1,512,2048]{3,2,1,0:T(8,128)(2,1)S(1)}, bf16[1,1,512,2048]{3,2,1,0:T(8,128)(2,1)}, u32[]{:S(2)}) copy-start(bf16[1,1,512,2048]{3,2,1,0:T(8,128)(2,1)} %param.9) | copy-start | bytes 6291460
  110.7 20.2 %all-to-all-start.3 = ((bf16[8,40,2048]{2,1,0:T(8,128)(2,1)}), bf16[8,40,2048]{2,1,0:T(8,128)(2,1)S(1)}, u32[]{:S(2)}, u32[]{:S(2)}) async-start(bf16[8,40,2048]{2,1,0:T(8,128)(2,1)} %bitcast.23), calls=%async_computation.3 | async-start | bytes 2621440 | tf_op jit(solution)/shard_map/all_to_all | solution.py:125
